TPU v7x, 256 devices: a whole 4x4x8 slice. The times are simulated.
256 devices in a mesh: group: 8 (over x, core), dev: 32 (over y, z).
Axes of the slice: x: 4, y: 4, z: 8, core: 2. Of those that a mesh axis runs over, the one named last changes fastest.
Arguments:
- em_image: bfloat16 [256, 1024, 512], P('group', 'dev'), may hold values from -6 to 6
- level_set: float32 [256, 1024, 512], P('group', 'dev'), may hold values from -6 to 6
- speeds: float32 [8], replicated, may hold values from -1 to 1.5
- brick_of_band: int32 [2048], P(('group', 'dev')), may hold values from 0 to 4095, as said below
- neighbours: int32 [4096, 6], P(('group', 'dev')), may hold values from -1 to 2047, as said below
- speed_index: int32 [4096], P(('group', 'dev')), may hold values from 0 to 7
Outputs:
- level_out: float32 [2048, 16, 16, 128], P(('group', 'dev'))
Inputs may be any that keep to these rules, and one draw needn't show every extreme that they name: `brick_of_band`: No brick is named twice. Band index j names a brick of the slab group of device j // 8. No device holds two bricks named by band indices that go to the same device j // 8. `neighbours`: entry k of brick b's list (sides x-, x+, y-, y+, z-, z+) is the band index j with brick_of_band[j] equal to the brick beside b on side k, or -1 where that side is the volume's boundary or the brick beside has no band index.
All inputs are finite; a program needn't handle non-finite values.
Results may differ from a plain program's by a relative error of at most 0.0003.
Values may be sent and summed in bfloat16 or wider, within the bound.
No kernel may reach another device: no remote copies, remote signals or barrier semaphores. Data moves between devices by JAX's collectives and lax.ppermute only.
A program may use at most 64 MiB of HBM per device.

v0:
```python
import math

import jax
import jax.numpy as jnp
from jax import lax
from jax.sharding import PartitionSpec as P

BX = 16
BY = 16
BZ = 128
BXN = 2
BYN = 2
BZN = 4
STEPS = 4


gauss_raw = [math.exp(-0.5 * position * position) for position in range(-2, 3)]
gauss_taps = [weight / sum(gauss_raw) for weight in gauss_raw]
time_step = 0.2
smoothing = 0.15
contrast = 0.02


def shortened(value):
    return jax.tree.map(lambda a: a.astype(jnp.bfloat16) if a.dtype == jnp.float32 else a, value)


def extended(cells, sides, width):
    for axis, dim in sides:
        count = lax.axis_size(axis)
        ends = count - 1
        head = lax.slice_in_dim(cells, 0, width, axis=dim)
        tail = lax.slice_in_dim(cells, cells.shape[dim] - width, cells.shape[dim], axis=dim)
        cells = jnp.concatenate(
            [
                lax.ppermute(tail, axis, [(i, (i + 1) % count) for i in range(ends)]),
                cells,
                lax.ppermute(head, axis, [((i + 1) % count, i) for i in range(ends)]),
            ],
            axis=dim,
        )
    return cells


def smooth_axis(values, along):
    length = values.shape[along] - 4
    summed = gauss_taps[0] * lax.slice_in_dim(values, 0, length, axis=along)
    for offset in range(1, 5):
        summed = summed + gauss_taps[offset] * lax.slice_in_dim(
            values, offset, offset + length, axis=along
        )
    return summed


def edge_map(window):
    smoothed = smooth_axis(smooth_axis(smooth_axis(window, 0), 1), 2)
    grad_x = (smoothed[2:, 1:-1, 1:-1] - smoothed[:-2, 1:-1, 1:-1]) * 0.5
    grad_y = (smoothed[1:-1, 2:, 1:-1] - smoothed[1:-1, :-2, 1:-1]) * 0.5
    grad_z = (smoothed[1:-1, 1:-1, 2:] - smoothed[1:-1, 1:-1, :-2]) * 0.5
    return 1.0 / (1.0 + (grad_x * grad_x + grad_y * grad_y + grad_z * grad_z) / contrast)


def to_bricks(block):
    shaped = block.reshape(BXN, BX, BYN, BY, BZN, BZ)
    return shaped.transpose(0, 2, 4, 1, 3, 5).reshape(BXN * BYN * BZN, BX, BY, BZ)


def own_faces(levels):
    side_faces = jnp.stack([levels[:, 0], levels[:, -1], levels[:, :, 0], levels[:, :, -1]], axis=1)
    end_faces = jnp.stack([levels[:, :, :, 0], levels[:, :, :, -1]], axis=1)
    return (side_faces, end_faces)


def advance(levels, side_ghost, end_ghost, edge_maps, speed_rows):
    with_z = jnp.concatenate(
        [end_ghost[:, 0][..., None], levels, end_ghost[:, 1][..., None]], axis=3
    )
    y_faces = jnp.pad(side_ghost[:, 2:4], ((0, 0), (0, 0), (0, 0), (1, 1)))
    with_y = jnp.concatenate(
        [y_faces[:, 0][:, :, None, :], with_z, y_faces[:, 1][:, :, None, :]], axis=2
    )
    x_faces = jnp.pad(side_ghost[:, 0:2], ((0, 0), (0, 0), (1, 1), (1, 1)))
    padded = jnp.concatenate([x_faces[:, 0][:, None], with_y, x_faces[:, 1][:, None]], axis=1)
    centre = padded[:, 1:-1, 1:-1, 1:-1]
    minus_x = padded[:, :-2, 1:-1, 1:-1]
    plus_x = padded[:, 2:, 1:-1, 1:-1]
    minus_y = padded[:, 1:-1, :-2, 1:-1]
    plus_y = padded[:, 1:-1, 2:, 1:-1]
    minus_z = padded[:, 1:-1, 1:-1, :-2]
    plus_z = padded[:, 1:-1, 1:-1, 2:]
    laplace = plus_x + minus_x + (plus_y + minus_y) + (plus_z + minus_z) - 6.0 * centre
    diff_x = (plus_x - minus_x) * 0.5
    diff_y = (plus_y - minus_y) * 0.5
    diff_z = (plus_z - minus_z) * 0.5
    gradient = diff_x * diff_x + diff_y * diff_y + diff_z * diff_z
    force = smoothing * laplace + speed_rows[:, None, None, None]
    return centre + time_step * edge_maps * force * jnp.sqrt(1.0 + gradient)


def assemble_ghosts(side_faces, end_faces, beside_lists):
    face_grid = side_faces.reshape((BXN, BYN, BZN) + side_faces.shape[1:])
    widened = extended(shortened(face_grid), (("group", 0), ("dev", 1)), 1).astype(face_grid.dtype)
    from_side = jnp.stack(
        [
            widened[:-2, 1:-1, :, 1],
            widened[2:, 1:-1, :, 0],
            widened[1:-1, :-2, :, 3],
            widened[1:-1, 2:, :, 2],
        ],
        axis=3,
    ).reshape(side_faces.shape)
    end_grid = end_faces.reshape((BXN, BYN, BZN) + end_faces.shape[1:])
    zero_faces = jnp.zeros_like(end_grid[:, :, :1, 0])
    lower_ghost = jnp.concatenate([zero_faces, end_grid[:, :, :-1, 1]], axis=2)
    upper_ghost = jnp.concatenate([end_grid[:, :, 1:, 0], zero_faces], axis=2)
    from_ends = jnp.stack([lower_ghost, upper_ghost], axis=3).reshape(end_faces.shape)
    linked = beside_lists >= 0
    side_ghost = jnp.where(linked[:, :4, None, None], from_side, side_faces)
    end_ghost = jnp.where(linked[:, 4:, None, None], from_ends, end_faces)
    return (side_ghost, end_ghost)


def place_rows(values, target, usable, partners):
    items = values.shape[0]
    matches = (target[None, :] == jnp.arange(partners)[:, None]) & usable[None, :]
    chosen = jnp.sum(jnp.where(matches, jnp.arange(items)[None, :], 0), axis=1)
    present = jnp.any(matches, axis=1)
    picked = jnp.take(values, chosen, axis=0)
    return jnp.where(
        present.reshape((partners,) + (1,) * (values.ndim - 1)), picked, jnp.zeros((), values.dtype)
    )


def per_device(em_image, level_set, speeds, brick_of_band, neighbours, speed_index):
    partners = lax.axis_size("dev")
    margin = extended(em_image, (("group", 0), ("dev", 1)), 3)
    window = jnp.pad(margin.astype(jnp.float32), ((0, 0), (0, 0), (3, 3)))
    edge_bricks = to_bricks(edge_map(window))
    level_bricks = to_bricks(level_set)
    bricks_here = level_bricks.shape[0]
    band_here = brick_of_band.shape[0]
    group_bands = lax.all_gather(brick_of_band, "dev", axis=0, tiled=True)
    device_here = lax.axis_index("group") * partners + lax.axis_index("dev")
    local_ids = device_here * bricks_here + jnp.arange(bricks_here, dtype=jnp.int32)
    found = group_bands[None, :] == local_ids[:, None]
    in_band = jnp.any(found, axis=1)
    band_place = jnp.sum(
        jnp.where(found, jnp.arange(group_bands.shape[0], dtype=jnp.int32)[None, :], 0), axis=1
    )
    owner_dev = band_place // band_here
    choose = speed_index[:, None] == jnp.arange(speeds.shape[0])[None, :]
    rates_here = jnp.sum(jnp.where(choose, speeds[None, :], 0.0), axis=1)
    source_dev = brick_of_band // bricks_here % partners
    every_slot = brick_of_band >= 0
    arrived = (
        lax.all_to_all(
            place_rows(level_bricks, owner_dev, in_band, partners),
            "dev",
            split_axis=0,
            concat_axis=0,
            tiled=True,
        ),
        lax.all_to_all(
            place_rows(edge_bricks, owner_dev, in_band, partners),
            "dev",
            split_axis=0,
            concat_axis=0,
            tiled=True,
        ),
        lax.all_to_all(
            place_rows(rates_here, owner_dev, in_band, partners),
            "dev",
            split_axis=0,
            concat_axis=0,
            tiled=True,
        ),
    )
    levels = jnp.take(arrived[0], source_dev, axis=0)
    edge_maps = jnp.take(arrived[1], source_dev, axis=0)
    speed_rows = jnp.take(arrived[2], source_dev, axis=0)
    for repeat in range(STEPS):
        side_faces, end_faces = own_faces(levels)
        homeward = (
            lax.all_to_all(
                shortened(place_rows(side_faces, source_dev, every_slot, partners)),
                "dev",
                split_axis=0,
                concat_axis=0,
                tiled=True,
            ),
            lax.all_to_all(
                shortened(place_rows(end_faces, source_dev, every_slot, partners)),
                "dev",
                split_axis=0,
                concat_axis=0,
                tiled=True,
            ),
        )
        side_ghost, end_ghost = assemble_ghosts(
            jnp.take(homeward[0], owner_dev, axis=0),
            jnp.take(homeward[1], owner_dev, axis=0),
            neighbours,
        )
        outward = (
            lax.all_to_all(
                shortened(place_rows(side_ghost, owner_dev, in_band, partners)),
                "dev",
                split_axis=0,
                concat_axis=0,
                tiled=True,
            ),
            lax.all_to_all(
                shortened(place_rows(end_ghost, owner_dev, in_band, partners)),
                "dev",
                split_axis=0,
                concat_axis=0,
                tiled=True,
            ),
        )
        levels = advance(
            levels,
            jnp.take(outward[0], source_dev, axis=0),
            jnp.take(outward[1], source_dev, axis=0),
            edge_maps,
            speed_rows,
        )
    return levels


def solution(mesh):
    placed = (
        P("group", "dev", None),
        P("group", "dev", None),
        P(),
        P(("group", "dev")),
        P(("group", "dev"), None),
        P(("group", "dev")),
    )
    return jax.shard_map(
        per_device,
        mesh=mesh,
        in_specs=placed,
        out_specs=P(("group", "dev"), None, None, None),
        check_vma=False,
    )
```

profile of v0, /device:TPU:1, one launch (start us, length us, event | category | flops | bytes accessed | tf_op | source)
XLA Modules:
  0.0 666.6 jit_solution(6263301415696498854)
XLA Ops:
  1.0 4.5 collective-permute-start
  10.2 19.2 %all-reduce.17 = s32[256]{0:T(256)S(1)} all-reduce(s32[256]{0:T(256)S(1)} %dynamic-update-slice), channel_id=1, replica_groups=mesh['group'=8,'dev'=32] {'dev'}, use_global_device_ids=true, to_apply=%add.17 | all-reduce | flops 256 | bytes 2048
  33.3 4.6 all-to-all-start.6
  37.9 2.9 reshape.464
  42.7 2.8 gather_fusion.2
  45.8 3.0 collective-permute-start.2
  50.9 3.8 collective-permute-done.3
  59.8 3.8 fusion.1
  63.6 3.2 fusion.21
  70.3 2.9 gather_fusion.4
  73.2 8.7 %select_select_fusion = (f32[32,16,16,128]{3,2,1,0:T(8,128)}, f32[32,16,16,128]{3,2,1,0:T(8,128)}) fusion(f32[32,16,16,128]{3,2,1,0:T(8,128)} %gather_fusion.4, pred[32]{0:T(512)(128)(4,1)S(1)} %compare_and_fusion.3, pred[32]{0:T(512)(128)(4,1)S(1)} %fusion.126, f32[32,16,16,128]{3,2,1,0:T(8,128)} %gather_fusion.2), kind=kLoop, calls=%fused_computation.40 | loop fusion | flops 4194304 | bytes 16777280 | tf_op jit(solution)/shard_map/jit(_where)/select_n | solution.py:129
  81.9 9.9 %all-to-all-start = ((f32[32,16,16,128]{3,2,1,0:T(8,128)}), f32[32,16,16,128]{3,2,1,0:T(8,128)}, u32[]{:S(2)}, u32[]{:S(2)}) async-start(f32[32,16,16,128]{3,2,1,0:T(8,128)} %get-tuple-element.106), calls=%async_computation | async-start | bytes 8388608 | tf_op jit(solution)/shard_map/all_to_all | solution.py:156
  93.7 88.8 %all-to-all-done = f32[32,16,16,128]{3,2,1,0:T(8,128)} async-done(((f32[32,16,16,128]{3,2,1,0:T(8,128)}), f32[32,16,16,128]{3,2,1,0:T(8,128)}, u32[]{:S(2)}, u32[]{:S(2)}) %all-to-all-start) | async-done | bytes 4194336 | tf_op jit(solution)/shard_map/all_to_all | solution.py:156
  182.6 2.8 gather_fusion.3
  189.0 8.5 %all-to-all-start.4 = ((bf16[32,2,256]{2,1,0:T(2,128)(2,1)}), bf16[32,2,256]{2,1,0:T(2,128)(2,1)S(1)}, u32[]{:S(2)}, u32[]{:S(2)}) async-start(bf16[32,2,256]{2,1,0:T(2,128)(2,1)} %reshape.923), calls=%async_computation.4 | async-start | bytes 65536 | tf_op jit(solution)/shard_map/all_to_all | solution.py:191
  197.7 8.5 %all-to-all-done.4 = bf16[32,2,256]{2,1,0:T(2,128)(2,1)S(1)} async-done(((bf16[32,2,256]{2,1,0:T(2,128)(2,1)}), bf16[32,2,256]{2,1,0:T(2,128)(2,1)S(1)}, u32[]{:S(2)}, u32[]{:S(2)}) %all-to-all-start.4) | async-done | bytes 32800 | tf_op jit(solution)/shard_map/all_to_all | solution.py:191
  206.3 14.7 %all_to_all.99 = bf16[32,4,16,128]{3,2,1,0:T(8,128)(2,1)S(1)} all-to-all(bf16[32,4,16,128]{3,2,1,0:T(8,128)(2,1)S(1)} %fusion.33), channel_id=1, replica_groups=mesh['group'=8,'dev'=32] {'dev'}, dimensions={0} | all-to-all | bytes 1048576 | tf_op jit(solution)/shard_map/all_to_all | solution.py:184
  221.0 7.3 %all-to-all-start.1 = ((f32[32,16,16,128]{3,2,1,0:T(8,128)}), f32[32,16,16,128]{3,2,1,0:T(8,128)}, u32[]{:S(2)}, u32[]{:S(2)}) async-start(f32[32,16,16,128]{3,2,1,0:T(8,128)} %get-tuple-element.105), calls=%async_computation.1 | async-start | bytes 8388608 | tf_op jit(solution)/shard_map/all_to_all | solution.py:163
  230.2 7.1 %collective-permute-start.4 = (bf16[1,2,4,4,16,128]{5,4,3,2,1,0:T(8,128)(2,1)S(1)}, bf16[1,2,4,4,16,128]{5,4,3,2,1,0:T(8,128)(2,1)S(1)}, u32[]{:S(2)}, u32[]{:S(2)}) collective-permute-start(bf16[1,2,4,4,16,128]{5,4,3,2,1,0:T(8,128)(2,1)S(1)} %bitcast.232), channel_id=1, source_target_pairs={{0,32},{32,64},{64,96},{96,128},{128,160},{160,192},{192,224},{1,3... | collective-permute-start | bytes 393224 | tf_op jit(solution)/shard_map/ppermute | solution.py:36
  239.2 4.7 collective-permute-done.5
  244.7 3.3 collective-permute-start.6
  251.2 69.0 %collective-permute-done.6 = bf16[4,1,4,4,16,128]{5,4,3,2,1,0:T(8,128)(2,1)S(1)} collective-permute-done((bf16[4,1,4,4,16,128]{5,4,3,2,1,0:T(8,128)(2,1)}, bf16[4,1,4,4,16,128]{5,4,3,2,1,0:T(8,128)(2,1)S(1)}, u32[]{:S(2)}, u32[]{:S(2)}) %collective-permute-start.6) | collective-permute-done | bytes 262176 | tf_op jit(solution)/shard_map/ppermute | solution.py:36
  320.2 4.0 collective-permute-done.7
  325.1 9.1 %all-to-all-start.5 = ((bf16[32,2,256]{2,1,0:T(2,128)(2,1)}), bf16[32,2,256]{2,1,0:T(2,128)(2,1)S(1)}, u32[]{:S(2)}, u32[]{:S(2)}) async-start(bf16[32,2,256]{2,1,0:T(2,128)(2,1)} %reshape.925), calls=%async_computation.5 | async-start | bytes 65536 | tf_op jit(solution)/shard_map/all_to_all | solution.py:212
  335.2 7.7 %all-to-all-done.5 = bf16[32,2,256]{2,1,0:T(2,128)(2,1)S(1)} async-done(((bf16[32,2,256]{2,1,0:T(2,128)(2,1)}), bf16[32,2,256]{2,1,0:T(2,128)(2,1)S(1)}, u32[]{:S(2)}, u32[]{:S(2)}) %all-to-all-start.5) | async-done | bytes 32800 | tf_op jit(solution)/shard_map/all_to_all | solution.py:212
  342.9 3.9 all-to-all-start.3
  346.8 2.9 gather_fusion.5
  354.4 4.6 all-to-all-done.3
  360.4 6.7 %multiply_add_fusion.3 = f32[8,16,16,128]{3,2,1,0:T(8,128)S(1)} fusion(f32[8,16,16,128]{3,2,1,0:T(8,128)S(1)} %broadcast_select_fusion, f32[8,16,16,1]{3,2,1,0:T(8,128)} %copy.253, f32[8,16,16,1]{3,2,1,0:T(8,128)} %copy.252, f32[8,16,1,130]{3,2,1,0:T(1,128)S(1)} %copy.255, f32[8,16,1,130]{3,2,1,0:T(1,128)S(1)} %copy.254, ...), kind=kLoop, calls=%fused_computation.182 | loop fusion | flops 11534336 | bytes 3445032 | tf_op jit(solution)/shard_map/add | solution.py:97
  370.5 7.8 %all-to-all-start.9 = ((bf16[32,2,256]{2,1,0:T(2,128)(2,1)}), bf16[32,2,256]{2,1,0:T(2,128)(2,1)S(1)}, u32[]{:S(2)}, u32[]{:S(2)}) async-start(bf16[32,2,256]{2,1,0:T(2,128)(2,1)} %reshape.927), calls=%async_computation.9 | async-start | bytes 65536 | tf_op jit(solution)/shard_map/all_to_all | solution.py:191
  379.3 7.7 %all-to-all-done.9 = bf16[32,2,256]{2,1,0:T(2,128)(2,1)S(1)} async-done(((bf16[32,2,256]{2,1,0:T(2,128)(2,1)}), bf16[32,2,256]{2,1,0:T(2,128)(2,1)S(1)}, u32[]{:S(2)}, u32[]{:S(2)}) %all-to-all-start.9) | async-done | bytes 32800 | tf_op jit(solution)/shard_map/all_to_all | solution.py:191
  387.1 3.9 all-to-all-start.7
  392.5 10.0 %all-to-all-done.7 = bf16[32,4,16,128]{3,2,1,0:T(8,128)(2,1)S(1)} async-done(((bf16[32,4,16,128]{3,2,1,0:T(8,128)(2,1)}), bf16[32,4,16,128]{3,2,1,0:T(8,128)(2,1)S(1)}, u32[]{:S(2)}, u32[]{:S(2)}) %all-to-all-start.7) | async-done | bytes 524320 | tf_op jit(solution)/shard_map/all_to_all | solution.py:184
  405.2 8.1 %collective-permute-start.9 = (bf16[1,2,4,4,16,128]{5,4,3,2,1,0:T(8,128)(2,1)S(1)}, bf16[1,2,4,4,16,128]{5,4,3,2,1,0:T(8,128)(2,1)S(1)}, u32[]{:S(2)}, u32[]{:S(2)}) collective-permute-start(bf16[1,2,4,4,16,128]{5,4,3,2,1,0:T(8,128)(2,1)S(1)} %bitcast.229), channel_id=1, source_target_pairs={{32,0},{64,32},{96,64},{128,96},{160,128},{192,160},{224,192},{33,... | collective-permute-start | bytes 393224 | tf_op jit(solution)/shard_map/ppermute | solution.py:38
  415.2 4.8 collective-permute-start.10
  424.4 5.3 all-to-all-start.10
  433.2 5.3 all-to-all-done.10
  438.5 3.9 all-to-all-start.8
  447.0 8.2 %all-to-all-done.8 = bf16[32,4,16,128]{3,2,1,0:T(8,128)(2,1)S(1)} async-done(((bf16[32,4,16,128]{3,2,1,0:T(8,128)(2,1)}), bf16[32,4,16,128]{3,2,1,0:T(8,128)(2,1)S(1)}, u32[]{:S(2)}, u32[]{:S(2)}) %all-to-all-start.8) | async-done | bytes 524320 | tf_op jit(solution)/shard_map/all_to_all | solution.py:205
  456.6 6.7 %multiply_add_fusion.2 = f32[8,16,16,128]{3,2,1,0:T(8,128)S(1)} fusion(f32[8,16,16,128]{3,2,1,0:T(8,128)S(1)} %multiply_add_fusion.3, f32[8,16,16,1]{3,2,1,0:T(8,128)} %copy.265, f32[8,16,16,1]{3,2,1,0:T(8,128)} %copy.264, f32[8,16,1,130]{3,2,1,0:T(1,128)S(1)} %copy.267, f32[8,16,1,130]{3,2,1,0:T(1,128)S(1)} %copy.266, ...), kind=kLoop, calls=%fused_computation.181 | loop fusion | flops 11534336 | bytes 3445032 | tf_op jit(solution)/shard_map/add | solution.py:97
  467.0 7.7 %all-to-all-start.13 = ((bf16[32,2,256]{2,1,0:T(2,128)(2,1)}), bf16[32,2,256]{2,1,0:T(2,128)(2,1)S(1)}, u32[]{:S(2)}, u32[]{:S(2)}) async-start(bf16[32,2,256]{2,1,0:T(2,128)(2,1)} %reshape.931), calls=%async_computation.13 | async-start | bytes 65536 | tf_op jit(solution)/shard_map/all_to_all | solution.py:191
  475.7 7.7 %all-to-all-done.13 = bf16[32,2,256]{2,1,0:T(2,128)(2,1)S(1)} async-done(((bf16[32,2,256]{2,1,0:T(2,128)(2,1)}), bf16[32,2,256]{2,1,0:T(2,128)(2,1)S(1)}, u32[]{:S(2)}, u32[]{:S(2)}) %all-to-all-start.13) | async-done | bytes 32800 | tf_op jit(solution)/shard_map/all_to_all | solution.py:191
  483.5 3.9 all-to-all-start.11
  489.0 10.0 %all-to-all-done.11 = bf16[32,4,16,128]{3,2,1,0:T(8,128)(2,1)S(1)} async-done(((bf16[32,4,16,128]{3,2,1,0:T(8,128)(2,1)}), bf16[32,4,16,128]{3,2,1,0:T(8,128)(2,1)S(1)}, u32[]{:S(2)}, u32[]{:S(2)}) %all-to-all-start.11) | async-done | bytes 524320 | tf_op jit(solution)/shard_map/all_to_all | solution.py:184
  499.9 6.1 collective-permute-start.12
  506.0 3.2 collective-permute-start.13
  513.2 3.6 collective-permute-start.14
  521.2 5.5 all-to-all-start.14
  530.3 5.2 all-to-all-done.14
  535.5 4.4 all-to-all-start.12
  544.5 9.1 %all-to-all-done.12 = bf16[32,4,16,128]{3,2,1,0:T(8,128)(2,1)S(1)} async-done(((bf16[32,4,16,128]{3,2,1,0:T(8,128)(2,1)}), bf16[32,4,16,128]{3,2,1,0:T(8,128)(2,1)S(1)}, u32[]{:S(2)}, u32[]{:S(2)}) %all-to-all-start.12) | async-done | bytes 524320 | tf_op jit(solution)/shard_map/all_to_all | solution.py:205
  554.9 6.7 %multiply_add_fusion.1 = f32[8,16,16,128]{3,2,1,0:T(8,128)S(1)} fusion(f32[8,16,16,128]{3,2,1,0:T(8,128)S(1)} %multiply_add_fusion.2, f32[8,16,16,1]{3,2,1,0:T(8,128)} %copy.276, f32[8,16,16,1]{3,2,1,0:T(8,128)} %copy.275, f32[8,16,1,130]{3,2,1,0:T(1,128)S(1)} %copy.278, f32[8,16,1,130]{3,2,1,0:T(1,128)S(1)} %copy.277, ...), kind=kLoop, calls=%fused_computation.180 | loop fusion | flops 11534336 | bytes 3445032 | tf_op jit(solution)/shard_map/add | solution.py:97
  565.3 8.0 %all-to-all-start.17 = ((bf16[32,2,256]{2,1,0:T(2,128)(2,1)}), bf16[32,2,256]{2,1,0:T(2,128)(2,1)S(1)}, u32[]{:S(2)}, u32[]{:S(2)}) async-start(bf16[32,2,256]{2,1,0:T(2,128)(2,1)} %reshape.935), calls=%async_computation.17 | async-start | bytes 65536 | tf_op jit(solution)/shard_map/all_to_all | solution.py:191
  574.4 7.7 %all-to-all-done.17 = bf16[32,2,256]{2,1,0:T(2,128)(2,1)S(1)} async-done(((bf16[32,2,256]{2,1,0:T(2,128)(2,1)}), bf16[32,2,256]{2,1,0:T(2,128)(2,1)S(1)}, u32[]{:S(2)}, u32[]{:S(2)}) %all-to-all-start.17) | async-done | bytes 32800 | tf_op jit(solution)/shard_map/all_to_all | solution.py:191
  582.1 3.9 all-to-all-start.15
  587.7 10.9 %all-to-all-done.15 = bf16[32,4,16,128]{3,2,1,0:T(8,128)(2,1)S(1)} async-done(((bf16[32,4,16,128]{3,2,1,0:T(8,128)(2,1)}), bf16[32,4,16,128]{3,2,1,0:T(8,128)(2,1)S(1)}, u32[]{:S(2)}, u32[]{:S(2)}) %all-to-all-start.15) | async-done | bytes 524320 | tf_op jit(solution)/shard_map/all_to_all | solution.py:184
  599.5 7.1 %collective-permute-start.16 = (bf16[1,2,4,4,16,128]{5,4,3,2,1,0:T(8,128)(2,1)S(1)}, bf16[1,2,4,4,16,128]{5,4,3,2,1,0:T(8,128)(2,1)S(1)}, u32[]{:S(2)}, u32[]{:S(2)}) collective-permute-start(bf16[1,2,4,4,16,128]{5,4,3,2,1,0:T(8,128)(2,1)S(1)} %bitcast.231), channel_id=1, source_target_pairs={{0,32},{32,64},{64,96},{96,128},{128,160},{160,192},{192,224},{1,3... | collective-permute-start | bytes 393224 | tf_op jit(solution)/shard_map/ppermute | solution.py:36
  609.4 3.5 collective-permute-done.17
  613.7 5.0 collective-permute-start.18
  623.2 5.5 all-to-all-start.18
  632.1 5.3 all-to-all-done.18
  637.4 4.8 all-to-all-start.16
  645.9 12.8 %all-to-all-done.16 = bf16[32,4,16,128]{3,2,1,0:T(8,128)(2,1)} async-done(((bf16[32,4,16,128]{3,2,1,0:T(8,128)(2,1)}), bf16[32,4,16,128]{3,2,1,0:T(8,128)(2,1)}, u32[]{:S(2)}, u32[]{:S(2)}) %all-to-all-start.16) | async-done | bytes 524320 | tf_op jit(solution)/shard_map/all_to_all | solution.py:205
  661.1 5.3 multiply_add_fusion
  (289 shorter events, 116.6 us)
Async XLA Ops:
  1.0 44.5 %collective-permute-start = (bf16[3,32,512]{2,1,0:T(8,128)(2,1)S(1)}, bf16[3,32,512]{2,1,0:T(8,128)(2,1)S(1)}, u32[]{:S(2)}, u32[]{:S(2)}) collective-permute-start(bf16[3,32,512]{2,1,0:T(8,128)(2,1)S(1)} %get-tuple-element.44), channel_id=1, source_target_pairs={{0,32},{32,64},{64,96},{96,128},{128,160},{160,192},{192,224},{1,3... | collective-permute-start | bytes 294920 | tf_op jit(solution)/shard_map/ppermute | solution.py:36
  5.5 40.2 %collective-permute-start.1 = (bf16[3,32,512]{2,1,0:T(8,128)(2,1)S(1)}, bf16[3,32,512]{2,1,0:T(8,128)(2,1)S(1)}, u32[]{:S(2)}, u32[]{:S(2)}) collective-permute-start(bf16[3,32,512]{2,1,0:T(8,128)(2,1)S(1)} %get-tuple-element.43), channel_id=1, source_target_pairs={{32,0},{64,32},{96,64},{128,96},{160,128},{192,160},{224,192},{33,... | collective-permute-start | bytes 294920 | tf_op jit(solution)/shard_map/ppermute | solution.py:38
  29.7 12.9 %copy-start.22 = (s32[16]{0:T(128)}, s32[16]{0:T(128)S(1)}, u32[]{:S(2)}) copy-start(s32[16]{0:T(128)S(1)} %get-tuple-element.26) | copy-start | bytes 196
  29.9 12.8 %copy-start.20 = (s32[32]{0:T(128)}, s32[32]{0:T(128)S(1)}, u32[]{:S(2)}) copy-start(s32[32]{0:T(128)S(1)} %select_reduce_fusion) | copy-start | bytes 388
  31.1 151.4 %copy-start.10 = (s32[1024]{0:T(1024)}, s32[1024]{0:T(1024)S(1)}, u32[]{:S(2)}) copy-start(s32[1024]{0:T(1024)S(1)} %get-tuple-element.108) | copy-start | bytes 12292
  33.3 48.6 %all-to-all-start.6 = ((f32[32,1,1]{2,1,0:T(1,128)}), f32[32,1,1]{2,1,0:T(1,128)}, u32[]{:S(2)}, u32[]{:S(2)}) async-start(f32[32,1,1]{2,1,0:T(1,128)} %copy.260), calls=%async_computation.6 | async-start | bytes 32768 | tf_op jit(solution)/shard_map/all_to_all | solution.py:170
  42.6 27.6 %copy-start.11 = (s32[1024]{0:T(1024)}, s32[1024]{0:T(1024)S(1)}, u32[]{:S(2)}) copy-start(s32[1024]{0:T(1024)S(1)} %pad_clamp_fusion.4) | copy-start | bytes 12292
  42.6 2.9 copy-start
  45.8 5.1 collective-permute-start.2
  48.8 6.0 collective-permute-start.3
  50.6 283.6 %copy-start.3 = (pred[32]{0:T(512)(128)(4,1)}, pred[32]{0:T(512)(128)(4,1)S(1)}, u32[]{:S(2)}) copy-start(pred[32]{0:T(512)(128)(4,1)S(1)} %compare_and_fusion.3) | copy-start | bytes 100
  81.9 9.9 %copy-start.21 = (s32[8]{0:T(128)S(1)}, s32[8]{0:T(128)}, u32[]{:S(2)}) copy-start(s32[8]{0:T(128)} %param.29) | copy-start | bytes 100
  81.9 9.9 %copy-start.19 = (s32[8]{0:T(128)S(1)}, s32[8]{0:T(128)}, u32[]{:S(2)}) copy-start(s32[8]{0:T(128)} %get-tuple-element.28) | copy-start | bytes 100
  81.9 100.7 %all-to-all-start = ((f32[32,16,16,128]{3,2,1,0:T(8,128)}), f32[32,16,16,128]{3,2,1,0:T(8,128)}, u32[]{:S(2)}, u32[]{:S(2)}) async-start(f32[32,16,16,128]{3,2,1,0:T(8,128)} %get-tuple-element.106), calls=%async_computation | async-start | bytes 8388608 | tf_op jit(solution)/shard_map/all_to_all | solution.py:156
  91.9 277.0 %copy-start.12 = (s32[1024]{0:T(1024)}, s32[1024]{0:T(1024)S(1)}, u32[]{:S(2)}) copy-start(s32[1024]{0:T(1024)S(1)} %pad_clamp_fusion.2) | copy-start | bytes 12292
  92.0 286.3 %copy-start.4 = (pred[32]{0:T(512)(128)(4,1)}, pred[32]{0:T(512)(128)(4,1)S(1)}, u32[]{:S(2)}) copy-start(pred[32]{0:T(512)(128)(4,1)S(1)} %fusion.128) | copy-start | bytes 100
  92.0 286.3 %copy-start.7 = (pred[32]{0:T(512)(128)(4,1)}, pred[32]{0:T(512)(128)(4,1)S(1)}, u32[]{:S(2)}) copy-start(pred[32]{0:T(512)(128)(4,1)S(1)} %compare_and_fusion.1) | copy-start | bytes 100
  93.7 266.7 %copy-start.14 = (f32[8]{0:T(128)}, f32[8]{0:T(128)S(1)}, u32[]{:S(2)}) copy-start(f32[8]{0:T(128)S(1)} %get-tuple-element.22) | copy-start | bytes 100
  189.0 17.3 %all-to-all-start.4 = ((bf16[32,2,256]{2,1,0:T(2,128)(2,1)}), bf16[32,2,256]{2,1,0:T(2,128)(2,1)S(1)}, u32[]{:S(2)}, u32[]{:S(2)}) async-start(bf16[32,2,256]{2,1,0:T(2,128)(2,1)} %reshape.923), calls=%async_computation.4 | async-start | bytes 65536 | tf_op jit(solution)/shard_map/all_to_all | solution.py:191
  220.9 7.3 %copy-start.18 = (s32[16,6]{0,1:T(8,128)S(1)}, s32[16,6]{0,1:T(8,128)}, u32[]{:S(2)}) copy-start(s32[16,6]{0,1:T(8,128)} %param.30) | copy-start | bytes 1156
  220.9 7.5 %copy-start.23 = (s32[16]{0:T(128)S(1)}, s32[16]{0:T(128)}, u32[]{:S(2)}) copy-start(s32[16]{0:T(128)} %copy-done.22) | copy-start | bytes 196
  221.0 104.2 %all-to-all-start.1 = ((f32[32,16,16,128]{3,2,1,0:T(8,128)}), f32[32,16,16,128]{3,2,1,0:T(8,128)}, u32[]{:S(2)}, u32[]{:S(2)}) async-start(f32[32,16,16,128]{3,2,1,0:T(8,128)} %get-tuple-element.105), calls=%async_computation.1 | async-start | bytes 8388608 | tf_op jit(solution)/shard_map/all_to_all | solution.py:163
  228.5 95.7 %copy-start.2 = (pred[16,2]{1,0:T(8,128)(4,1)}, pred[16,2]{1,0:T(8,128)(4,1)S(1)}, u32[]{:S(2)}) copy-start(pred[16,2]{1,0:T(8,128)(4,1)S(1)} %copy.249) | copy-start | bytes 100
  228.5 174.0 %copy-start.13 = (s32[1024]{0:T(1024)}, s32[1024]{0:T(1024)S(1)}, u32[]{:S(2)}) copy-start(s32[1024]{0:T(1024)S(1)} %pad_clamp_fusion.1) | copy-start | bytes 12292
  230.2 9.1 %collective-permute-start.4 = (bf16[1,2,4,4,16,128]{5,4,3,2,1,0:T(8,128)(2,1)S(1)}, bf16[1,2,4,4,16,128]{5,4,3,2,1,0:T(8,128)(2,1)S(1)}, u32[]{:S(2)}, u32[]{:S(2)}) collective-permute-start(bf16[1,2,4,4,16,128]{5,4,3,2,1,0:T(8,128)(2,1)S(1)} %bitcast.232), channel_id=1, source_target_pairs={{0,32},{32,64},{64,96},{96,128},{128,160},{160,192},{192,224},{1,3... | collective-permute-start | bytes 393224 | tf_op jit(solution)/shard_map/ppermute | solution.py:36
  237.2 6.7 %collective-permute-start.5 = (bf16[1,2,4,4,16,128]{5,4,3,2,1,0:T(8,128)(2,1)S(1)}, bf16[1,2,4,4,16,128]{5,4,3,2,1,0:T(8,128)(2,1)S(1)}, u32[]{:S(2)}, u32[]{:S(2)}) collective-permute-start(bf16[1,2,4,4,16,128]{5,4,3,2,1,0:T(8,128)(2,1)S(1)} %bitcast.228), channel_id=1, source_target_pairs={{32,0},{64,32},{96,64},{128,96},{160,128},{192,160},{224,192},{33,... | collective-permute-start | bytes 393224 | tf_op jit(solution)/shard_map/ppermute | solution.py:38
  244.7 75.5 %collective-permute-start.6 = (bf16[4,1,4,4,16,128]{5,4,3,2,1,0:T(8,128)(2,1)}, bf16[4,1,4,4,16,128]{5,4,3,2,1,0:T(8,128)(2,1)S(1)}, u32[]{:S(2)}, u32[]{:S(2)}) collective-permute-start(bf16[4,1,4,4,16,128]{5,4,3,2,1,0:T(8,128)(2,1)} %get-tuple-element.55), channel_id=1, source_target_pairs={{0,1},{1,2},{2,3},{3,4},{4,5},{5,6},{6,7},{7,8},{8,9},{9,10},{10,1... | collective-permute-start | bytes 786440 | tf_op jit(solution)/shard_map/ppermute | solution.py:36
  248.1 76.1 %collective-permute-start.7 = (bf16[4,1,4,4,16,128]{5,4,3,2,1,0:T(8,128)(2,1)S(1)}, bf16[4,1,4,4,16,128]{5,4,3,2,1,0:T(8,128)(2,1)S(1)}, u32[]{:S(2)}, u32[]{:S(2)}) collective-permute-start(bf16[4,1,4,4,16,128]{5,4,3,2,1,0:T(8,128)(2,1)S(1)} %get-tuple-element.56), channel_id=1, source_target_pairs={{1,0},{2,1},{3,2},{4,3},{5,4},{6,5},{7,6},{8,7},{9,8},{10,9},{11,1... | collective-permute-start | bytes 786440 | tf_op jit(solution)/shard_map/ppermute | solution.py:38
  325.1 17.8 %all-to-all-start.5 = ((bf16[32,2,256]{2,1,0:T(2,128)(2,1)}), bf16[32,2,256]{2,1,0:T(2,128)(2,1)S(1)}, u32[]{:S(2)}, u32[]{:S(2)}) async-start(bf16[32,2,256]{2,1,0:T(2,128)(2,1)} %reshape.925), calls=%async_computation.5 | async-start | bytes 65536 | tf_op jit(solution)/shard_map/all_to_all | solution.py:212
  342.9 16.1 %all-to-all-start.3 = ((bf16[32,4,16,128]{3,2,1,0:T(8,128)(2,1)}), bf16[32,4,16,128]{3,2,1,0:T(8,128)(2,1)S(1)}, u32[]{:S(2)}, u32[]{:S(2)}) async-start(bf16[32,4,16,128]{3,2,1,0:T(8,128)(2,1)} %select_select_fusion.13), calls=%async_computation.3 | async-start | bytes 1048576 | tf_op jit(solution)/shard_map/all_to_all | solution.py:205
  370.5 16.6 %all-to-all-start.9 = ((bf16[32,2,256]{2,1,0:T(2,128)(2,1)}), bf16[32,2,256]{2,1,0:T(2,128)(2,1)S(1)}, u32[]{:S(2)}, u32[]{:S(2)}) async-start(bf16[32,2,256]{2,1,0:T(2,128)(2,1)} %reshape.927), calls=%async_computation.9 | async-start | bytes 65536 | tf_op jit(solution)/shard_map/all_to_all | solution.py:191
  387.1 15.4 %all-to-all-start.7 = ((bf16[32,4,16,128]{3,2,1,0:T(8,128)(2,1)}), bf16[32,4,16,128]{3,2,1,0:T(8,128)(2,1)S(1)}, u32[]{:S(2)}, u32[]{:S(2)}) async-start(bf16[32,4,16,128]{3,2,1,0:T(8,128)(2,1)} %fusion.32), calls=%async_computation.7 | async-start | bytes 1048576 | tf_op jit(solution)/shard_map/all_to_all | solution.py:184
  403.2 10.9 %collective-permute-start.8 = (bf16[1,2,4,4,16,128]{5,4,3,2,1,0:T(8,128)(2,1)S(1)}, bf16[1,2,4,4,16,128]{5,4,3,2,1,0:T(8,128)(2,1)S(1)}, u32[]{:S(2)}, u32[]{:S(2)}) collective-permute-start(bf16[1,2,4,4,16,128]{5,4,3,2,1,0:T(8,128)(2,1)S(1)} %bitcast.233), channel_id=1, source_target_pairs={{0,32},{32,64},{64,96},{96,128},{128,160},{160,192},{192,224},{1,3... | collective-permute-start | bytes 393224 | tf_op jit(solution)/shard_map/ppermute | solution.py:36
  405.2 9.1 %collective-permute-start.9 = (bf16[1,2,4,4,16,128]{5,4,3,2,1,0:T(8,128)(2,1)S(1)}, bf16[1,2,4,4,16,128]{5,4,3,2,1,0:T(8,128)(2,1)S(1)}, u32[]{:S(2)}, u32[]{:S(2)}) collective-permute-start(bf16[1,2,4,4,16,128]{5,4,3,2,1,0:T(8,128)(2,1)S(1)} %bitcast.229), channel_id=1, source_target_pairs={{32,0},{64,32},{96,64},{128,96},{160,128},{192,160},{224,192},{33,... | collective-permute-start | bytes 393224 | tf_op jit(solution)/shard_map/ppermute | solution.py:38
  415.2 14.5 %collective-permute-start.10 = (bf16[4,1,4,4,16,128]{5,4,3,2,1,0:T(8,128)(2,1)}, bf16[4,1,4,4,16,128]{5,4,3,2,1,0:T(8,128)(2,1)}, u32[]{:S(2)}, u32[]{:S(2)}) collective-permute-start(bf16[4,1,4,4,16,128]{5,4,3,2,1,0:T(8,128)(2,1)} %get-tuple-element.53), channel_id=1, source_target_pairs={{0,1},{1,2},{2,3},{3,4},{4,5},{5,6},{6,7},{7,8},{8,9},{9,10},{10,1... | collective-permute-start | bytes 786440 | tf_op jit(solution)/shard_map/ppermute | solution.py:36
  420.0 9.7 %collective-permute-start.11 = (bf16[4,1,4,4,16,128]{5,4,3,2,1,0:T(8,128)(2,1)}, bf16[4,1,4,4,16,128]{5,4,3,2,1,0:T(8,128)(2,1)}, u32[]{:S(2)}, u32[]{:S(2)}) collective-permute-start(bf16[4,1,4,4,16,128]{5,4,3,2,1,0:T(8,128)(2,1)} %get-tuple-element.54), channel_id=1, source_target_pairs={{1,0},{2,1},{3,2},{4,3},{5,4},{6,5},{7,6},{8,7},{9,8},{10,9},{11,1... | collective-permute-start | bytes 786440 | tf_op jit(solution)/shard_map/ppermute | solution.py:38
  424.4 14.1 %all-to-all-start.10 = ((bf16[32,2,256]{2,1,0:T(2,128)(2,1)}), bf16[32,2,256]{2,1,0:T(2,128)(2,1)S(1)}, u32[]{:S(2)}, u32[]{:S(2)}) async-start(bf16[32,2,256]{2,1,0:T(2,128)(2,1)} %reshape.929), calls=%async_computation.10 | async-start | bytes 65536 | tf_op jit(solution)/shard_map/all_to_all | solution.py:212
  431.6 25.0 %copy-start.15 = (f32[8]{0:T(128)S(1)}, f32[8]{0:T(128)}, u32[]{:S(2)}) copy-start(f32[8]{0:T(128)} %copy-done.14) | copy-start | bytes 100
  438.5 16.8 %all-to-all-start.8 = ((bf16[32,4,16,128]{3,2,1,0:T(8,128)(2,1)}), bf16[32,4,16,128]{3,2,1,0:T(8,128)(2,1)S(1)}, u32[]{:S(2)}, u32[]{:S(2)}) async-start(bf16[32,4,16,128]{3,2,1,0:T(8,128)(2,1)} %select_select_fusion.11), calls=%async_computation.8 | async-start | bytes 1048576 | tf_op jit(solution)/shard_map/all_to_all | solution.py:205
  463.3 2.7 copy-start.5
  463.3 2.7 copy-start.8
  467.0 16.4 %all-to-all-start.13 = ((bf16[32,2,256]{2,1,0:T(2,128)(2,1)}), bf16[32,2,256]{2,1,0:T(2,128)(2,1)S(1)}, u32[]{:S(2)}, u32[]{:S(2)}) async-start(bf16[32,2,256]{2,1,0:T(2,128)(2,1)} %reshape.931), calls=%async_computation.13 | async-start | bytes 65536 | tf_op jit(solution)/shard_map/all_to_all | solution.py:191
  483.5 15.5 %all-to-all-start.11 = ((bf16[32,4,16,128]{3,2,1,0:T(8,128)(2,1)}), bf16[32,4,16,128]{3,2,1,0:T(8,128)(2,1)S(1)}, u32[]{:S(2)}, u32[]{:S(2)}) async-start(bf16[32,4,16,128]{3,2,1,0:T(8,128)(2,1)} %fusion.31), calls=%async_computation.11 | async-start | bytes 1048576 | tf_op jit(solution)/shard_map/all_to_all | solution.py:184
  499.9 10.2 %collective-permute-start.12 = (bf16[1,2,4,4,16,128]{5,4,3,2,1,0:T(8,128)(2,1)S(1)}, bf16[1,2,4,4,16,128]{5,4,3,2,1,0:T(8,128)(2,1)S(1)}, u32[]{:S(2)}, u32[]{:S(2)}) collective-permute-start(bf16[1,2,4,4,16,128]{5,4,3,2,1,0:T(8,128)(2,1)S(1)} %bitcast.234), channel_id=1, source_target_pairs={{0,32},{32,64},{64,96},{96,128},{128,160},{160,192},{192,224},{1,3... | collective-permute-start | bytes 393224 | tf_op jit(solution)/shard_map/ppermute | solution.py:36
  506.0 6.3 collective-permute-start.13
  512.3 6.7 copy-start.1
  513.2 13.5 %collective-permute-start.14 = (bf16[4,1,4,4,16,128]{5,4,3,2,1,0:T(8,128)(2,1)}, bf16[4,1,4,4,16,128]{5,4,3,2,1,0:T(8,128)(2,1)}, u32[]{:S(2)}, u32[]{:S(2)}) collective-permute-start(bf16[4,1,4,4,16,128]{5,4,3,2,1,0:T(8,128)(2,1)} %get-tuple-element.51), channel_id=1, source_target_pairs={{0,1},{1,2},{2,3},{3,4},{4,5},{5,6},{6,7},{7,8},{8,9},{9,10},{10,1... | collective-permute-start | bytes 786440 | tf_op jit(solution)/shard_map/ppermute | solution.py:36
  516.9 10.0 %collective-permute-start.15 = (bf16[4,1,4,4,16,128]{5,4,3,2,1,0:T(8,128)(2,1)}, bf16[4,1,4,4,16,128]{5,4,3,2,1,0:T(8,128)(2,1)}, u32[]{:S(2)}, u32[]{:S(2)}) collective-permute-start(bf16[4,1,4,4,16,128]{5,4,3,2,1,0:T(8,128)(2,1)} %get-tuple-element.52), channel_id=1, source_target_pairs={{1,0},{2,1},{3,2},{4,3},{5,4},{6,5},{7,6},{8,7},{9,8},{10,9},{11,1... | collective-permute-start | bytes 786440 | tf_op jit(solution)/shard_map/ppermute | solution.py:38
  521.2 14.3 %all-to-all-start.14 = ((bf16[32,2,256]{2,1,0:T(2,128)(2,1)}), bf16[32,2,256]{2,1,0:T(2,128)(2,1)S(1)}, u32[]{:S(2)}, u32[]{:S(2)}) async-start(bf16[32,2,256]{2,1,0:T(2,128)(2,1)} %reshape.933), calls=%async_computation.14 | async-start | bytes 65536 | tf_op jit(solution)/shard_map/all_to_all | solution.py:212
  528.8 26.2 %copy-start.16 = (f32[8]{0:T(128)S(1)}, f32[8]{0:T(128)}, u32[]{:S(2)}) copy-start(f32[8]{0:T(128)} %copy-done.14) | copy-start | bytes 100
  535.5 18.1 %all-to-all-start.12 = ((bf16[32,4,16,128]{3,2,1,0:T(8,128)(2,1)}), bf16[32,4,16,128]{3,2,1,0:T(8,128)(2,1)S(1)}, u32[]{:S(2)}, u32[]{:S(2)}) async-start(bf16[32,4,16,128]{3,2,1,0:T(8,128)(2,1)} %select_select_fusion.9), calls=%async_computation.12 | async-start | bytes 1048576 | tf_op jit(solution)/shard_map/all_to_all | solution.py:205
  561.6 2.7 copy-start.6
  561.6 2.7 copy-start.9
  565.3 16.8 %all-to-all-start.17 = ((bf16[32,2,256]{2,1,0:T(2,128)(2,1)}), bf16[32,2,256]{2,1,0:T(2,128)(2,1)S(1)}, u32[]{:S(2)}, u32[]{:S(2)}) async-start(bf16[32,2,256]{2,1,0:T(2,128)(2,1)} %reshape.935), calls=%async_computation.17 | async-start | bytes 65536 | tf_op jit(solution)/shard_map/all_to_all | solution.py:191
  582.1 16.5 %all-to-all-start.15 = ((bf16[32,4,16,128]{3,2,1,0:T(8,128)(2,1)}), bf16[32,4,16,128]{3,2,1,0:T(8,128)(2,1)S(1)}, u32[]{:S(2)}, u32[]{:S(2)}) async-start(bf16[32,4,16,128]{3,2,1,0:T(8,128)(2,1)} %fusion.30), calls=%async_computation.15 | async-start | bytes 1048576 | tf_op jit(solution)/shard_map/all_to_all | solution.py:184
  599.5 9.9 %collective-permute-start.16 = (bf16[1,2,4,4,16,128]{5,4,3,2,1,0:T(8,128)(2,1)S(1)}, bf16[1,2,4,4,16,128]{5,4,3,2,1,0:T(8,128)(2,1)S(1)}, u32[]{:S(2)}, u32[]{:S(2)}) collective-permute-start(bf16[1,2,4,4,16,128]{5,4,3,2,1,0:T(8,128)(2,1)S(1)} %bitcast.231), channel_id=1, source_target_pairs={{0,32},{32,64},{64,96},{96,128},{128,160},{160,192},{192,224},{1,3... | collective-permute-start | bytes 393224 | tf_op jit(solution)/shard_map/ppermute | solution.py:36
  606.5 6.3 collective-permute-start.17
  613.7 14.9 %collective-permute-start.18 = (bf16[4,1,4,4,16,128]{5,4,3,2,1,0:T(8,128)(2,1)}, bf16[4,1,4,4,16,128]{5,4,3,2,1,0:T(8,128)(2,1)}, u32[]{:S(2)}, u32[]{:S(2)}) collective-permute-start(bf16[4,1,4,4,16,128]{5,4,3,2,1,0:T(8,128)(2,1)} %get-tuple-element.49), channel_id=1, source_target_pairs={{0,1},{1,2},{2,3},{3,4},{4,5},{5,6},{6,7},{7,8},{8,9},{9,10},{10,1... | collective-permute-start | bytes 786440 | tf_op jit(solution)/shard_map/ppermute | solution.py:36
  618.8 9.9 %collective-permute-start.19 = (bf16[4,1,4,4,16,128]{5,4,3,2,1,0:T(8,128)(2,1)}, bf16[4,1,4,4,16,128]{5,4,3,2,1,0:T(8,128)(2,1)}, u32[]{:S(2)}, u32[]{:S(2)}) collective-permute-start(bf16[4,1,4,4,16,128]{5,4,3,2,1,0:T(8,128)(2,1)} %get-tuple-element.50), channel_id=1, source_target_pairs={{1,0},{2,1},{3,2},{4,3},{5,4},{6,5},{7,6},{8,7},{9,8},{10,9},{11,1... | collective-permute-start | bytes 786440 | tf_op jit(solution)/shard_map/ppermute | solution.py:38
  623.2 14.2 %all-to-all-start.18 = ((bf16[32,2,256]{2,1,0:T(2,128)(2,1)}), bf16[32,2,256]{2,1,0:T(2,128)(2,1)S(1)}, u32[]{:S(2)}, u32[]{:S(2)}) async-start(bf16[32,2,256]{2,1,0:T(2,128)(2,1)} %reshape.937), calls=%async_computation.18 | async-start | bytes 65536 | tf_op jit(solution)/shard_map/all_to_all | solution.py:212
  630.6 30.5 %copy-start.17 = (f32[8]{0:T(128)S(1)}, f32[8]{0:T(128)}, u32[]{:S(2)}) copy-start(f32[8]{0:T(128)} %copy-done.14) | copy-start | bytes 100
  637.4 21.3 %all-to-all-start.16 = ((bf16[32,4,16,128]{3,2,1,0:T(8,128)(2,1)}), bf16[32,4,16,128]{3,2,1,0:T(8,128)(2,1)}, u32[]{:S(2)}, u32[]{:S(2)}) async-start(bf16[32,4,16,128]{3,2,1,0:T(8,128)(2,1)} %select_select_fusion.7), calls=%async_computation.16 | async-start | bytes 1048576 | tf_op jit(solution)/shard_map/all_to_all | solution.py:205
where the time goes:
time: 678 us; the launch traced here: 667 us
  waiting for transfers between devices  297 us (44%)
  starting transfers between devices  178 us (26%)
  local copies, waits for them, and re-layouts  82.1 us (12%)
  other arithmetic  73 us (11%)
  blocking collectives  33.8 us (5%)
    all_to_all x1, waiting for transfers between devices, per_device(): lax.all_to_all(place_rows(level_bricks, owner_dev, in_band, partners), 'd...  88.8 us
    ppermute x10, waiting for transfers between devices, extended(): lax.ppermute(tail, axis, [(i, (i + 1) % count) for i in range(ends)])  69.3 us
    ppermute x10, starting transfers between devices, extended(): lax.ppermute(tail, axis, [(i, (i + 1) % count) for i in range(ends)])  46.5 us
    all_to_all x4, waiting for transfers between devices, per_device(): lax.all_to_all(shortened(place_rows(side_ghost, owner_dev, in_band, partn...  34.8 us
    all_to_all x4, starting transfers between devices, per_device(): lax.all_to_all(shortened(place_rows(end_faces, source_dev, every_slot, pa...  31.9 us
    all_to_all x4, waiting for transfers between devices, per_device(): lax.all_to_all(shortened(place_rows(end_faces, source_dev, every_slot, pa...  31.7 us
    all_to_all x3, waiting for transfers between devices, per_device(): lax.all_to_all(shortened(place_rows(side_faces, source_dev, every_slot, p...  30.9 us
    add x4, other arithmetic, advance(): return centre + time_step * edge_maps * force * jnp.sqrt(1.0 + gradient)  25.4 us
  transfers between devices with their start and end apart: 38, of which 25 were waited for; matrix products, arithmetic and copies ran while one was open for 15% of the time, Pallas kernels for 0%

commit v1 on v0

--- a/solution.py
+++ b/solution.py
@@ -131,13 +131,70 @@
     )
 
 
+def halo_planes(cells, axis, dim):
+    count = lax.axis_size(axis)
+    ends = count - 1
+    head = lax.slice_in_dim(cells, 0, 1, axis=dim)
+    tail = lax.slice_in_dim(cells, cells.shape[dim] - 1, cells.shape[dim], axis=dim)
+    from_below = lax.ppermute(tail, axis, [(i, i + 1) for i in range(ends)])
+    from_above = lax.ppermute(head, axis, [(i + 1, i) for i in range(ends)])
+    return from_below, from_above
+
+
+def brick_field(per_brick, shape):
+    grid = per_brick.reshape(BXN, 1, BYN, 1, BZN, 1)
+    grid = jnp.broadcast_to(grid, (BXN, BX, BYN, BY, BZN, BZ))
+    return grid.reshape(shape)
+
+
+def dense_step(lvl, edge, rate, uses):
+    below_x, above_x = halo_planes(lvl, "group", 0)
+    below_y, above_y = halo_planes(lvl, "dev", 1)
+    zero_z = jnp.zeros_like(lvl[:, :, :1])
+    shifted = (
+        jnp.concatenate([below_x, lvl[:-1]], axis=0),
+        jnp.concatenate([lvl[1:], above_x], axis=0),
+        jnp.concatenate([below_y, lvl[:, :-1]], axis=1),
+        jnp.concatenate([lvl[:, 1:], above_y], axis=1),
+        jnp.concatenate([zero_z, lvl[:, :, :-1]], axis=2),
+        jnp.concatenate([lvl[:, :, 1:], zero_z], axis=2),
+    )
+    minus_x, plus_x, minus_y, plus_y, minus_z, plus_z = (
+        jnp.where(use, value, lvl) for use, value in zip(uses, shifted)
+    )
+    centre = lvl
+    laplace = plus_x + minus_x + (plus_y + minus_y) + (plus_z + minus_z) - 6.0 * centre
+    diff_x = (plus_x - minus_x) * 0.5
+    diff_y = (plus_y - minus_y) * 0.5
+    diff_z = (plus_z - minus_z) * 0.5
+    gradient = diff_x * diff_x + diff_y * diff_y + diff_z * diff_z
+    force = smoothing * laplace + rate
+    return centre + time_step * edge * force * jnp.sqrt(1.0 + gradient)
+
+
 def per_device(em_image, level_set, speeds, brick_of_band, neighbours, speed_index):
     partners = lax.axis_size("dev")
     margin = extended(em_image, (("group", 0), ("dev", 1)), 3)
     window = jnp.pad(margin.astype(jnp.float32), ((0, 0), (0, 0), (3, 3)))
-    edge_bricks = to_bricks(edge_map(window))
-    level_bricks = to_bricks(level_set)
-    bricks_here = level_bricks.shape[0]
+    edge = edge_map(window)
+    shape = level_set.shape
+    bricks_here = BXN * BYN * BZN
+    choose = speed_index[:, None] == jnp.arange(speeds.shape[0])[None, :]
+    rates_here = jnp.sum(jnp.where(choose, speeds[None, :], 0.0), axis=1)
+    rate = brick_field(rates_here, shape)
+    linked = neighbours >= 0
+    sizes = (BX, BX, BY, BY, BZ, BZ)
+    axes = (0, 0, 1, 1, 2, 2)
+    uses = []
+    for side in range(6):
+        link = brick_field(linked[:, side], shape)
+        pos = lax.broadcasted_iota(jnp.int32, shape, axes[side]) % sizes[side]
+        inner = pos != (0 if side % 2 == 0 else sizes[side] - 1)
+        uses.append(inner | link)
+    lvl = level_set
+    for repeat in range(STEPS):
+        lvl = dense_step(lvl, edge, rate, uses)
+    level_bricks = to_bricks(lvl)
     band_here = brick_of_band.shape[0]
     group_bands = lax.all_gather(brick_of_band, "dev", axis=0, tiled=True)
     device_here = lax.axis_index("group") * partners + lax.axis_index("dev")
@@ -148,83 +205,15 @@
         jnp.where(found, jnp.arange(group_bands.shape[0], dtype=jnp.int32)[None, :], 0), axis=1
     )
     owner_dev = band_place // band_here
-    choose = speed_index[:, None] == jnp.arange(speeds.shape[0])[None, :]
-    rates_here = jnp.sum(jnp.where(choose, speeds[None, :], 0.0), axis=1)
     source_dev = brick_of_band // bricks_here % partners
-    every_slot = brick_of_band >= 0
-    arrived = (
-        lax.all_to_all(
-            place_rows(level_bricks, owner_dev, in_band, partners),
-            "dev",
-            split_axis=0,
-            concat_axis=0,
-            tiled=True,
-        ),
-        lax.all_to_all(
-            place_rows(edge_bricks, owner_dev, in_band, partners),
-            "dev",
-            split_axis=0,
-            concat_axis=0,
-            tiled=True,
-        ),
-        lax.all_to_all(
-            place_rows(rates_here, owner_dev, in_band, partners),
-            "dev",
-            split_axis=0,
-            concat_axis=0,
-            tiled=True,
-        ),
-    )
-    levels = jnp.take(arrived[0], source_dev, axis=0)
-    edge_maps = jnp.take(arrived[1], source_dev, axis=0)
-    speed_rows = jnp.take(arrived[2], source_dev, axis=0)
-    for repeat in range(STEPS):
-        side_faces, end_faces = own_faces(levels)
-        homeward = (
-            lax.all_to_all(
-                shortened(place_rows(side_faces, source_dev, every_slot, partners)),
-                "dev",
-                split_axis=0,
-                concat_axis=0,
-                tiled=True,
-            ),
-            lax.all_to_all(
-                shortened(place_rows(end_faces, source_dev, every_slot, partners)),
-                "dev",
-                split_axis=0,
-                concat_axis=0,
-                tiled=True,
-            ),
-        )
-        side_ghost, end_ghost = assemble_ghosts(
-            jnp.take(homeward[0], owner_dev, axis=0),
-            jnp.take(homeward[1], owner_dev, axis=0),
-            neighbours,
-        )
-        outward = (
-            lax.all_to_all(
-                shortened(place_rows(side_ghost, owner_dev, in_band, partners)),
-                "dev",
-                split_axis=0,
-                concat_axis=0,
-                tiled=True,
-            ),
-            lax.all_to_all(
-                shortened(place_rows(end_ghost, owner_dev, in_band, partners)),
-                "dev",
-                split_axis=0,
-                concat_axis=0,
-                tiled=True,
-            ),
-        )
-        levels = advance(
-            levels,
-            jnp.take(outward[0], source_dev, axis=0),
-            jnp.take(outward[1], source_dev, axis=0),
-            edge_maps,
-            speed_rows,
-        )
-    return levels
+    arrived = lax.all_to_all(
+        place_rows(level_bricks, owner_dev, in_band, partners),
+        "dev",
+        split_axis=0,
+        concat_axis=0,
+        tiled=True,
+    )
+    return jnp.take(arrived, source_dev, axis=0)
 
 
 def solution(mesh):

time: 678 us -> 307 us (0.45); the launches traced: 667 us -> 305 us
  waiting for transfers between devices: 297 us -> 102 us
  starting transfers between devices: 178 us -> 74.8 us
  other arithmetic: 73 us -> 48.1 us
  local copies, waits for them, and re-layouts: 82.1 us -> 58.3 us
  blocking collectives: 33.8 us -> 21.3 us
    all_to_all x17 -> x0, waiting for transfers between devices: 121 us -> none  [the longest x4 34.8 us: per_device(): lax.all_to_all(shortened(place_rows(side_ghost, owner_dev, in_band, partn...]
    all_to_all x17 -> x0, starting transfers between devices: 97.8 us -> none  [the longest x4 31.9 us: per_device(): lax.all_to_all(shortened(place_rows(end_faces, source_dev, every_slot, pa...]
    ppermute x10 -> x2, waiting for transfers between devices: 69.3 us -> 0.01 us  [extended(): lax.ppermute(tail, axis, [(i, (i + 1) % count) for i in range(ends)])]
    ppermute x0 -> x16, starting transfers between devices: none -> 50.7 us  [the longest x8 32.2 us: halo_planes(): from_below = lax.ppermute(tail, axis, [(i, i + 1) for i in range(ends)])]
    ppermute x10 -> x2, starting transfers between devices: 46.5 us -> 8.26 us  [extended(): lax.ppermute(tail, axis, [(i, (i + 1) % count) for i in range(ends)])]
    ppermute x10 -> x2, starting transfers between devices: 23.5 us -> 3.2 us  [extended(): lax.ppermute(head, axis, [((i + 1) % count, i) for i in range(ends)])]
    ppermute x10 -> x2, waiting for transfers between devices: 18.3 us -> 0.01 us  [extended(): lax.ppermute(head, axis, [((i + 1) % count, i) for i in range(ends)])]
    slice x16 -> x21, local copies, waits for them, and re-layouts: 4.39 us -> 20.4 us  [the longest x4 6.76 us: dense_step(): lvl[:, 1:]]
  transfers between devices with their start and end apart: 38 -> 21, of which waited for: 25 -> 4; matrix products, arithmetic and copies ran while one was open for 15% -> 19% of each run, Pallas kernels for 0% -> 0%
where the time goes in v1:
time: 307 us; the launch traced here: 305 us
  waiting for transfers between devices  102 us (33%)
  starting transfers between devices  74.8 us (24%)
  local copies, waits for them, and re-layouts  58.3 us (19%)
  other arithmetic  48.1 us (16%)
  blocking collectives  21.3 us (7%)
    all_to_all x1, waiting for transfers between devices, per_device(): lax.all_to_all(place_rows(level_bricks, owner_dev, in_band, partners), 'd...  99.5 us
    ppermute x8, starting transfers between devices, halo_planes(): from_below = lax.ppermute(tail, axis, [(i, i + 1) for i in range(ends)])  32.2 us
    add x4, other arithmetic, dense_step(): return centre + time_step * edge * force * jnp.sqrt(1.0 + gradient)  25.5 us
    unnamed x1, blocking collectives  21.3 us
    ppermute x8, starting transfers between devices, halo_planes(): from_above = lax.ppermute(head, axis, [(i + 1, i) for i in range(ends)])  18.5 us
    reshape x7, local copies, waits for them, and re-layouts, brick_field(): return grid.reshape(shape)  13.5 us
    all_to_all x1, starting transfers between devices, per_device(): lax.all_to_all(place_rows(level_bricks, owner_dev, in_band, partners), 'd...  12.6 us
    broadcast_in_dim x14, local copies, waits for them, and re-layouts, brick_field(): grid = jnp.broadcast_to(grid, (BXN, BX, BYN, BY, BZN, BZ))  9.26 us
  transfers between devices with their start and end apart: 21, of which 4 were waited for; matrix products, arithmetic and copies ran while one was open for 19% of the time, Pallas kernels for 0%

profile of v1, /device:TPU:1, one launch (start us, length us, event | category | flops | bytes accessed | tf_op | source)
XLA Modules:
  0.0 305.4 jit_solution(4608925916448364635)
XLA Ops:
  0.0 1.0 fusion.68
  1.0 4.5 %collective-permute-start = (bf16[3,32,512]{2,1,0:T(8,128)(2,1)S(1)}, bf16[3,32,512]{2,1,0:T(8,128)(2,1)S(1)}, u32[]{:S(2)}, u32[]{:S(2)}) collective-permute-start(bf16[3,32,512]{2,1,0:T(8,128)(2,1)S(1)} %get-tuple-element.58), channel_id=1, source_target_pairs={{0,32},{32,64},{64,96},{96,128},{128,160},{160,192},{192,224},{1,3... | collective-permute-start | bytes 294920 | tf_op jit(solution)/shard_map/ppermute | solution.py:36
  5.5 1.9 collective-permute-start.1
  7.4 1.5 fusion.63
  8.9 1.9 collective-permute-start.4
  10.8 3.6 %collective-permute-start.5 = (f32[1,32,512]{2,1,0:T(8,128)}, f32[1,32,512]{2,1,0:T(8,128)}, u32[]{:S(2)}, u32[]{:S(2)}) collective-permute-start(f32[1,32,512]{2,1,0:T(8,128)} %get-tuple-element.48), channel_id=1, source_target_pairs={{0,32},{32,64},{64,96},{96,128},{128,160},{160,192},{192,224},{1,3... | collective-permute-start | bytes 196616 | tf_op jit(solution)/shard_map/ppermute | solution.py:139
  14.5 2.0 fusion.65
  16.4 1.3 collective-permute-start.6
  17.8 5.1 %fusion.64 = (f32[32,31,512]{2,1,0:T(8,128)}, f32[32,31,512]{2,1,0:T(8,128)}) fusion(f32[32,32,512]{2,1,0:T(8,128)} %param.7), kind=kLoop, calls=%fused_computation.152 | loop fusion | bytes 8126464 | tf_op jit(solution)/shard_map/slice | solution.py:158
  22.9 2.8 fusion.66
  25.7 2.4 fusion.62
  28.6 1.3 dynamic-slice
  31.1 1.3 dynamic-update-slice
  32.5 21.3 %all-reduce.9 = s32[256]{0:T(256)} all-reduce(s32[256]{0:T(256)} %dynamic-update-slice), channel_id=1, replica_groups=mesh['group'=8,'dev'=32] {'dev'}, use_global_device_ids=true, to_apply=%add.9 | all-reduce | flops 256 | bytes 2048
  53.8 0.9 fusion.37
  54.6 0.9 compare_reduce_fusion
  58.5 1.3 select_reduce_fusion.1
  60.4 1.0 copy-done.7
  61.6 3.8 %collective-permute-start.2 = (bf16[38,3,512]{2,1,0:T(4,128)(2,1)S(1)}, bf16[38,3,512]{2,1,0:T(4,128)(2,1)}, u32[]{:S(2)}, u32[]{:S(2)}) collective-permute-start(bf16[38,3,512]{2,1,0:T(4,128)(2,1)S(1)} %get-tuple-element.55), channel_id=1, source_target_pairs={{0,1},{1,2},{2,3},{3,4},{4,5},{5,6},{6,7},{7,8},{8,9},{9,10},{10,1... | collective-permute-start | bytes 350216 | tf_op jit(solution)/shard_map/ppermute | solution.py:36
  65.3 1.3 collective-permute-start.3
  67.8 1.3 broadcast_in_dim.139
  69.1 1.4 reshape.86
  70.6 1.3 broadcast_in_dim.141
  71.9 2.1 reshape.87
  74.1 1.3 broadcast_in_dim.143
  75.4 2.1 reshape.88
  77.6 1.3 broadcast_in_dim.145
  78.9 2.1 reshape.89
  81.1 1.3 broadcast_in_dim.147
  82.3 2.1 reshape.90
  84.5 1.8 broadcast_in_dim.151
  86.4 3.1 %reshape.91 = f32[32,32,512]{2,1,0:T(8,128)} reshape(f32[2,16,2,16,4,128]{5,4,3,2,1,0:T(4,128)} %broadcast_in_dim.151) | data formatting | bytes 4194304 | tf_op jit(solution)/shard_map/reshape | solution.py:147
  89.6 4.2 %collective-permute-start.7 = (f32[32,1,512]{2,1,0:T(1,128)S(1)}, f32[32,1,512]{2,1,0:T(1,128)S(1)}, u32[]{:S(2)}, u32[]{:S(2)}) collective-permute-start(f32[32,1,512]{2,1,0:T(1,128)S(1)} %copy-done.9), channel_id=1, source_target_pairs={{0,1},{1,2},{2,3},{3,4},{4,5},{5,6},{6,7},{7,8},{8,9},{9,10},{10,1... | collective-permute-start | bytes 196616 | tf_op jit(solution)/shard_map/ppermute | solution.py:139
  93.8 3.1 %fusion.36 = f32[38,38,518]{2,1,0:T(8,128)S(1)} fusion(bf16[38,3,512]{2,1,0:T(4,128)(2,1)} %collective-permute-done.3, bf16[38,32,512]{2,1,0:T(8,128)(2,1)} %copy-done.7, bf16[38,3,512]{2,1,0:T(4,128)(2,1)} %collective-permute-done.2), kind=kLoop, calls=%fused_computation.85 | loop fusion | flops 8975904 | bytes 4470624 | tf_op jit(solution)/shard_map/jit(_pad)/pad | solution.py:178
  96.9 1.3 fusion.9
  98.3 2.0 fusion.5
  100.3 3.8 %fusion.1 = f32[34,34,514]{2,1,0:T(8,128)S(1)} fusion(f32[34,34,518]{2,1,0:T(8,128)S(1)} %fusion.5), kind=kLoop, calls=%fused_computation.7 | loop fusion | flops 5347656 | bytes 14260416 | tf_op jit(solution)/shard_map/add | solution.py:49
  104.2 10.6 %multiply_add_fusion.3 = (f32[32,32,512]{2,1,0:T(8,128)S(1)}, f32[32,32,512]{2,1,0:T(8,128)}) fusion(f32[32,32,512]{2,1,0:T(8,128)S(1)} %copy-done, f32[32,32,512]{2,1,0:T(8,128)S(1)} %copy-done.1, f32[32,32,511]{2,1,0:T(8,128)} %get-tuple-element.54, f32[32,32,511]{2,1,0:T(8,128)} %get-tuple-element.53, f32[32,31,512]{2,1,0:T(8,128)} %get-tuple-element.50, ...), kind=kLoop, calls=%fused_computation.75 | loop fusion | flops 33554432 | bytes 36699648 | tf_op jit(solution)/shard_map/add | solution.py:172
  115.3 0.8 fusion.61
  116.3 1.3 collective-permute-start.10
  117.6 4.0 %collective-permute-start.11 = (f32[32,1,512]{2,1,0:T(1,128)S(1)}, f32[32,1,512]{2,1,0:T(1,128)S(1)}, u32[]{:S(2)}, u32[]{:S(2)}) collective-permute-start(f32[32,1,512]{2,1,0:T(1,128)S(1)} %get-tuple-element.42), channel_id=1, source_target_pairs={{0,1},{1,2},{2,3},{3,4},{4,5},{5,6},{6,7},{7,8},{8,9},{9,10},{10,1... | collective-permute-start | bytes 196616 | tf_op jit(solution)/shard_map/ppermute | solution.py:139
  121.6 7.6 %collective-permute-start.8 = (f32[1,32,512]{2,1,0:T(8,128)S(1)}, f32[1,32,512]{2,1,0:T(8,128)S(1)}, u32[]{:S(2)}, u32[]{:S(2)}) collective-permute-start(f32[1,32,512]{2,1,0:T(8,128)S(1)} %get-tuple-element.37), channel_id=1, source_target_pairs={{32,0},{64,32},{96,64},{128,96},{160,128},{192,160},{224,192},{33,... | collective-permute-start | bytes 196616 | tf_op jit(solution)/shard_map/ppermute | solution.py:140
  129.2 3.2 %collective-permute-start.9 = (f32[1,32,512]{2,1,0:T(8,128)S(1)}, f32[1,32,512]{2,1,0:T(8,128)S(1)}, u32[]{:S(2)}, u32[]{:S(2)}) collective-permute-start(f32[1,32,512]{2,1,0:T(8,128)S(1)} %get-tuple-element.38), channel_id=1, source_target_pairs={{0,32},{32,64},{64,96},{96,128},{128,160},{160,192},{192,224},{1,3... | collective-permute-start | bytes 196616 | tf_op jit(solution)/shard_map/ppermute | solution.py:139
  133.7 5.0 %multiply_add_fusion.2 = f32[32,32,512]{2,1,0:T(8,128)S(1)} fusion(f32[32,32,512]{2,1,0:T(8,128)S(1)} %get-tuple-element.13, f32[32,32,512]{2,1,0:T(8,128)S(1)} %copy-done.2, f32[32,32,512]{2,1,0:T(8,128)S(1)} %copy-done.1, f32[32,32,511]{2,1,0:T(8,128)S(1)} %get-tuple-element.44, f32[32,32,511]{2,1,0:T(8,128)S(1)} %get-tuple-element.43, ...), kind=kLoop, calls=%fused_computation.74 | loop fusion | flops 25690112 | bytes 24113952 | tf_op jit(solution)/shard_map/add | solution.py:172
  139.3 0.8 fusion.56
  140.2 1.9 collective-permute-start.12
  142.1 4.3 %collective-permute-start.13 = (f32[1,32,512]{2,1,0:T(8,128)S(1)}, f32[1,32,512]{2,1,0:T(8,128)S(1)}, u32[]{:S(2)}, u32[]{:S(2)}) collective-permute-start(f32[1,32,512]{2,1,0:T(8,128)S(1)} %get-tuple-element.28), channel_id=1, source_target_pairs={{0,32},{32,64},{64,96},{96,128},{128,160},{160,192},{192,224},{1,3... | collective-permute-start | bytes 196616 | tf_op jit(solution)/shard_map/ppermute | solution.py:139
  146.4 1.3 collective-permute-start.14
  147.7 4.2 %collective-permute-start.15 = (f32[32,1,512]{2,1,0:T(1,128)S(1)}, f32[32,1,512]{2,1,0:T(1,128)S(1)}, u32[]{:S(2)}, u32[]{:S(2)}) collective-permute-start(f32[32,1,512]{2,1,0:T(1,128)S(1)} %get-tuple-element.32), channel_id=1, source_target_pairs={{0,1},{1,2},{2,3},{3,4},{4,5},{5,6},{6,7},{7,8},{8,9},{9,10},{10,1... | collective-permute-start | bytes 196616 | tf_op jit(solution)/shard_map/ppermute | solution.py:139
  153.0 5.0 %multiply_add_fusion.1 = f32[32,32,512]{2,1,0:T(8,128)S(1)} fusion(f32[32,32,512]{2,1,0:T(8,128)S(1)} %multiply_add_fusion.2, f32[32,32,512]{2,1,0:T(8,128)S(1)} %copy-done.2, f32[32,32,512]{2,1,0:T(8,128)S(1)} %copy-done.1, f32[32,32,511]{2,1,0:T(8,128)S(1)} %get-tuple-element.34, f32[32,32,511]{2,1,0:T(8,128)S(1)} %get-tuple-element.33, ...), kind=kLoop, calls=%fused_computation.73 | loop fusion | flops 25690112 | bytes 24113952 | tf_op jit(solution)/shard_map/add | solution.py:172
  158.5 0.8 fusion.51
  159.5 1.9 collective-permute-start.16
  161.4 4.0 %collective-permute-start.17 = (f32[1,32,512]{2,1,0:T(8,128)S(1)}, f32[1,32,512]{2,1,0:T(8,128)S(1)}, u32[]{:S(2)}, u32[]{:S(2)}) collective-permute-start(f32[1,32,512]{2,1,0:T(8,128)S(1)} %get-tuple-element.18), channel_id=1, source_target_pairs={{0,32},{32,64},{64,96},{96,128},{128,160},{160,192},{192,224},{1,3... | collective-permute-start | bytes 196616 | tf_op jit(solution)/shard_map/ppermute | solution.py:139
  165.4 1.3 collective-permute-start.18
  166.7 4.7 %collective-permute-start.19 = (f32[32,1,512]{2,1,0:T(1,128)S(1)}, f32[32,1,512]{2,1,0:T(1,128)S(1)}, u32[]{:S(2)}, u32[]{:S(2)}) collective-permute-start(f32[32,1,512]{2,1,0:T(1,128)S(1)} %get-tuple-element.22), channel_id=1, source_target_pairs={{0,1},{1,2},{2,3},{3,4},{4,5},{5,6},{6,7},{7,8},{8,9},{9,10},{10,1... | collective-permute-start | bytes 196616 | tf_op jit(solution)/shard_map/ppermute | solution.py:139
  172.8 4.9 %multiply_add_fusion = f32[32,32,512]{2,1,0:T(8,128)S(1)} fusion(f32[32,32,512]{2,1,0:T(8,128)S(1)} %multiply_add_fusion.1, f32[32,32,512]{2,1,0:T(8,128)S(1)} %copy-done.2, f32[32,32,512]{2,1,0:T(8,128)S(1)} %copy-done.1, f32[32,32,511]{2,1,0:T(8,128)S(1)} %get-tuple-element.24, f32[32,32,511]{2,1,0:T(8,128)S(1)} %get-tuple-element.23, ...), kind=kLoop, calls=%fused_computation.72 | loop fusion | flops 25690112 | bytes 24113952 | tf_op jit(solution)/shard_map/add | solution.py:172
  177.7 1.7 reshape.92
  179.4 1.8 copy.8
  181.3 2.9 gather_fusion
  184.2 5.1 %select_select_fusion = f32[32,16,16,128]{3,2,1,0:T(8,128)} fusion(f32[32,16,16,128]{3,2,1,0:T(8,128)} %gather_fusion, pred[32]{0:T(512)(128)(4,1)S(1)} %copy-done.11, pred[32]{0:T(512)(128)(4,1)S(1)} %fusion.39), kind=kLoop, calls=%fused_computation.4 | loop fusion | flops 2097152 | bytes 8388672 | tf_op jit(solution)/shard_map/jit(_where)/select_n | solution.py:129
  189.2 12.6 %all-to-all-start = ((f32[32,16,16,128]{3,2,1,0:T(8,128)}), f32[32,16,16,128]{3,2,1,0:T(8,128)}, u32[]{:S(2)}, u32[]{:S(2)}) async-start(f32[32,16,16,128]{3,2,1,0:T(8,128)} %select_select_fusion), calls=%async_computation | async-start | bytes 8388608 | tf_op jit(solution)/shard_map/all_to_all | solution.py:209
  201.9 99.5 %all-to-all-done = f32[32,16,16,128]{3,2,1,0:T(8,128)} async-done(((f32[32,16,16,128]{3,2,1,0:T(8,128)}), f32[32,16,16,128]{3,2,1,0:T(8,128)}, u32[]{:S(2)}, u32[]{:S(2)}) %all-to-all-start) | async-done | bytes 4194336 | tf_op jit(solution)/shard_map/all_to_all | solution.py:209
  301.4 2.8 gather_fusion.1
  304.2 1.1 broadcast_select_fusion
  (108 shorter events, 12.2 us)
Async XLA Ops:
  1.0 59.3 %collective-permute-start = (bf16[3,32,512]{2,1,0:T(8,128)(2,1)S(1)}, bf16[3,32,512]{2,1,0:T(8,128)(2,1)S(1)}, u32[]{:S(2)}, u32[]{:S(2)}) collective-permute-start(bf16[3,32,512]{2,1,0:T(8,128)(2,1)S(1)} %get-tuple-element.58), channel_id=1, source_target_pairs={{0,32},{32,64},{64,96},{96,128},{128,160},{160,192},{192,224},{1,3... | collective-permute-start | bytes 294920 | tf_op jit(solution)/shard_map/ppermute | solution.py:36
  5.5 54.9 %collective-permute-start.1 = (bf16[3,32,512]{2,1,0:T(8,128)(2,1)S(1)}, bf16[3,32,512]{2,1,0:T(8,128)(2,1)S(1)}, u32[]{:S(2)}, u32[]{:S(2)}) collective-permute-start(bf16[3,32,512]{2,1,0:T(8,128)(2,1)S(1)} %get-tuple-element.57), channel_id=1, source_target_pairs={{32,0},{64,32},{96,64},{128,96},{160,128},{192,160},{224,192},{33,... | collective-permute-start | bytes 294920 | tf_op jit(solution)/shard_map/ppermute | solution.py:38
  8.9 95.2 %collective-permute-start.4 = (f32[1,32,512]{2,1,0:T(8,128)}, f32[1,32,512]{2,1,0:T(8,128)}, u32[]{:S(2)}, u32[]{:S(2)}) collective-permute-start(f32[1,32,512]{2,1,0:T(8,128)} %get-tuple-element.47), channel_id=1, source_target_pairs={{32,0},{64,32},{96,64},{128,96},{160,128},{192,160},{224,192},{33,... | collective-permute-start | bytes 196616 | tf_op jit(solution)/shard_map/ppermute | solution.py:140
  10.8 93.2 %collective-permute-start.5 = (f32[1,32,512]{2,1,0:T(8,128)}, f32[1,32,512]{2,1,0:T(8,128)}, u32[]{:S(2)}, u32[]{:S(2)}) collective-permute-start(f32[1,32,512]{2,1,0:T(8,128)} %get-tuple-element.48), channel_id=1, source_target_pairs={{0,32},{32,64},{64,96},{96,128},{128,160},{160,192},{192,224},{1,3... | collective-permute-start | bytes 196616 | tf_op jit(solution)/shard_map/ppermute | solution.py:139
  16.4 87.6 %collective-permute-start.6 = (f32[32,1,512]{2,1,0:T(1,128)}, f32[32,1,512]{2,1,0:T(1,128)}, u32[]{:S(2)}, u32[]{:S(2)}) collective-permute-start(f32[32,1,512]{2,1,0:T(1,128)} %get-tuple-element.51), channel_id=1, source_target_pairs={{1,0},{2,1},{3,2},{4,3},{5,4},{6,5},{7,6},{8,7},{9,8},{10,9},{11,1... | collective-permute-start | bytes 196616 | tf_op jit(solution)/shard_map/ppermute | solution.py:140
  17.8 5.2 %copy-start = (f32[32,32,512]{2,1,0:T(8,128)S(1)}, f32[32,32,512]{2,1,0:T(8,128)}, u32[]{:S(2)}) copy-start(f32[32,32,512]{2,1,0:T(8,128)} %param.7) | copy-start | bytes 6291460
  25.7 34.6 %copy-start.8 = (bf16[32,32,512]{2,1,0:T(8,128)(2,1)S(1)}, bf16[32,32,512]{2,1,0:T(8,128)(2,1)}, u32[]{:S(2)}) copy-start(bf16[32,32,512]{2,1,0:T(8,128)(2,1)} %param.6) | copy-start | bytes 3145732
  55.5 0.5 copy-start.19
  55.5 4.7 %copy-start.22 = (s32[16]{0:T(128)}, s32[16]{0:T(128)S(1)}, u32[]{:S(2)}) copy-start(s32[16]{0:T(128)S(1)} %and_select_fusion) | copy-start | bytes 196
  60.3 6.4 %copy-start.18 = (pred[16]{0:T(512)(128)(4,1)S(1)}, pred[16]{0:T(512)(128)(4,1)}, u32[]{:S(2)}) copy-start(pred[16]{0:T(512)(128)(4,1)} %get-tuple-element.5) | copy-start | bytes 52
  60.3 7.5 %copy-start.17 = (pred[16]{0:T(512)(128)(4,1)S(1)}, pred[16]{0:T(512)(128)(4,1)}, u32[]{:S(2)}) copy-start(pred[16]{0:T(512)(128)(4,1)} %get-tuple-element.10) | copy-start | bytes 52
  60.4 10.2 %copy-start.16 = (pred[16]{0:T(512)(128)(4,1)S(1)}, pred[16]{0:T(512)(128)(4,1)}, u32[]{:S(2)}) copy-start(pred[16]{0:T(512)(128)(4,1)} %get-tuple-element.9) | copy-start | bytes 52
  60.4 1.0 copy-start.7
  61.6 28.0 %collective-permute-start.2 = (bf16[38,3,512]{2,1,0:T(4,128)(2,1)S(1)}, bf16[38,3,512]{2,1,0:T(4,128)(2,1)}, u32[]{:S(2)}, u32[]{:S(2)}) collective-permute-start(bf16[38,3,512]{2,1,0:T(4,128)(2,1)S(1)} %get-tuple-element.55), channel_id=1, source_target_pairs={{0,1},{1,2},{2,3},{3,4},{4,5},{5,6},{6,7},{7,8},{8,9},{9,10},{10,1... | collective-permute-start | bytes 350216 | tf_op jit(solution)/shard_map/ppermute | solution.py:36
  65.3 28.4 %collective-permute-start.3 = (bf16[38,3,512]{2,1,0:T(4,128)(2,1)S(1)}, bf16[38,3,512]{2,1,0:T(4,128)(2,1)}, u32[]{:S(2)}, u32[]{:S(2)}) collective-permute-start(bf16[38,3,512]{2,1,0:T(4,128)(2,1)S(1)} %get-tuple-element.56), channel_id=1, source_target_pairs={{1,0},{2,1},{3,2},{4,3},{5,4},{6,5},{7,6},{8,7},{9,8},{10,9},{11,1... | collective-permute-start | bytes 350216 | tf_op jit(solution)/shard_map/ppermute | solution.py:38
  67.2 6.8 %copy-start.15 = (pred[16]{0:T(512)(128)(4,1)S(1)}, pred[16]{0:T(512)(128)(4,1)}, u32[]{:S(2)}) copy-start(pred[16]{0:T(512)(128)(4,1)} %get-tuple-element.8) | copy-start | bytes 52
  69.1 8.4 %copy-start.14 = (pred[16]{0:T(512)(128)(4,1)S(1)}, pred[16]{0:T(512)(128)(4,1)}, u32[]{:S(2)}) copy-start(pred[16]{0:T(512)(128)(4,1)} %get-tuple-element.7) | copy-start | bytes 52
  71.9 9.1 %copy-start.13 = (pred[16]{0:T(512)(128)(4,1)S(1)}, pred[16]{0:T(512)(128)(4,1)}, u32[]{:S(2)}) copy-start(pred[16]{0:T(512)(128)(4,1)} %get-tuple-element.6) | copy-start | bytes 52
  75.4 9.1 %copy-start.12 = (f32[16]{0:T(128)S(1)}, f32[16]{0:T(128)}, u32[]{:S(2)}) copy-start(f32[16]{0:T(128)} %select_reduce_fusion.1) | copy-start | bytes 196
  86.4 3.1 %copy-start.20 = (pred[16]{0:T(512)(128)(4,1)S(1)}, pred[16]{0:T(512)(128)(4,1)}, u32[]{:S(2)}) copy-start(pred[16]{0:T(512)(128)(4,1)} %copy-done.19) | copy-start | bytes 52
  86.4 3.1 %copy-start.23 = (s32[16]{0:T(128)S(1)}, s32[16]{0:T(128)}, u32[]{:S(2)}) copy-start(s32[16]{0:T(128)} %copy-done.22) | copy-start | bytes 196
  86.4 3.2 %copy-start.9 = (f32[32,1,512]{2,1,0:T(1,128)S(1)}, f32[32,1,512]{2,1,0:T(1,128)}, u32[]{:S(2)}) copy-start(f32[32,1,512]{2,1,0:T(1,128)} %get-tuple-element.52) | copy-start | bytes 196612
  89.6 14.5 %collective-permute-start.7 = (f32[32,1,512]{2,1,0:T(1,128)S(1)}, f32[32,1,512]{2,1,0:T(1,128)S(1)}, u32[]{:S(2)}, u32[]{:S(2)}) collective-permute-start(f32[32,1,512]{2,1,0:T(1,128)S(1)} %copy-done.9), channel_id=1, source_target_pairs={{0,1},{1,2},{2,3},{3,4},{4,5},{5,6},{6,7},{7,8},{8,9},{9,10},{10,1... | collective-permute-start | bytes 196616 | tf_op jit(solution)/shard_map/ppermute | solution.py:139
  100.2 3.9 %copy-start.1 = (f32[32,32,512]{2,1,0:T(8,128)S(1)}, f32[32,32,512]{2,1,0:T(8,128)}, u32[]{:S(2)}) copy-start(f32[32,32,512]{2,1,0:T(8,128)} %reshape.91) | copy-start | bytes 6291460
  100.3 3.9 %copy-start.3 = (pred[32,32,512]{2,1,0:T(8,128)(4,1)S(1)}, pred[32,32,512]{2,1,0:T(8,128)(4,1)}, u32[]{:S(2)}) copy-start(pred[32,32,512]{2,1,0:T(8,128)(4,1)} %reshape.87) | copy-start | bytes 1572868
  100.3 3.9 %copy-start.4 = (pred[32,32,512]{2,1,0:T(8,128)(4,1)S(1)}, pred[32,32,512]{2,1,0:T(8,128)(4,1)}, u32[]{:S(2)}) copy-start(pred[32,32,512]{2,1,0:T(8,128)(4,1)} %reshape.88) | copy-start | bytes 1572868
  100.3 3.9 %copy-start.5 = (pred[32,32,512]{2,1,0:T(8,128)(4,1)S(1)}, pred[32,32,512]{2,1,0:T(8,128)(4,1)}, u32[]{:S(2)}) copy-start(pred[32,32,512]{2,1,0:T(8,128)(4,1)} %reshape.89) | copy-start | bytes 1572868
  100.3 3.9 %copy-start.10 = (pred[32]{0:T(512)(128)(4,1)S(1)}, pred[32]{0:T(512)(128)(4,1)}, u32[]{:S(2)}) copy-start(pred[32]{0:T(512)(128)(4,1)} %compare_and_fusion) | copy-start | bytes 100
  116.3 16.7 %collective-permute-start.10 = (f32[32,1,512]{2,1,0:T(1,128)S(1)}, f32[32,1,512]{2,1,0:T(1,128)S(1)}, u32[]{:S(2)}, u32[]{:S(2)}) collective-permute-start(f32[32,1,512]{2,1,0:T(1,128)S(1)} %get-tuple-element.41), channel_id=1, source_target_pairs={{1,0},{2,1},{3,2},{4,3},{5,4},{6,5},{7,6},{8,7},{9,8},{10,9},{11,1... | collective-permute-start | bytes 196616 | tf_op jit(solution)/shard_map/ppermute | solution.py:140
  117.6 15.4 %collective-permute-start.11 = (f32[32,1,512]{2,1,0:T(1,128)S(1)}, f32[32,1,512]{2,1,0:T(1,128)S(1)}, u32[]{:S(2)}, u32[]{:S(2)}) collective-permute-start(f32[32,1,512]{2,1,0:T(1,128)S(1)} %get-tuple-element.42), channel_id=1, source_target_pairs={{0,1},{1,2},{2,3},{3,4},{4,5},{5,6},{6,7},{7,8},{8,9},{9,10},{10,1... | collective-permute-start | bytes 196616 | tf_op jit(solution)/shard_map/ppermute | solution.py:139
  121.6 11.4 %collective-permute-start.8 = (f32[1,32,512]{2,1,0:T(8,128)S(1)}, f32[1,32,512]{2,1,0:T(8,128)S(1)}, u32[]{:S(2)}, u32[]{:S(2)}) collective-permute-start(f32[1,32,512]{2,1,0:T(8,128)S(1)} %get-tuple-element.37), channel_id=1, source_target_pairs={{32,0},{64,32},{96,64},{128,96},{160,128},{192,160},{224,192},{33,... | collective-permute-start | bytes 196616 | tf_op jit(solution)/shard_map/ppermute | solution.py:140
  129.2 4.5 %copy-start.2 = (f32[32,32,512]{2,1,0:T(8,128)S(1)}, f32[32,32,512]{2,1,0:T(8,128)}, u32[]{:S(2)}) copy-start(f32[32,32,512]{2,1,0:T(8,128)} %get-tuple-element.14) | copy-start | bytes 6291460
  129.2 4.5 %copy-start.6 = (pred[32,32,512]{2,1,0:T(8,128)(4,1)S(1)}, pred[32,32,512]{2,1,0:T(8,128)(4,1)}, u32[]{:S(2)}) copy-start(pred[32,32,512]{2,1,0:T(8,128)(4,1)} %reshape.90) | copy-start | bytes 1572868
  129.2 4.5 %collective-permute-start.9 = (f32[1,32,512]{2,1,0:T(8,128)S(1)}, f32[1,32,512]{2,1,0:T(8,128)S(1)}, u32[]{:S(2)}, u32[]{:S(2)}) collective-permute-start(f32[1,32,512]{2,1,0:T(8,128)S(1)} %get-tuple-element.38), channel_id=1, source_target_pairs={{0,32},{32,64},{64,96},{96,128},{128,160},{160,192},{192,224},{1,3... | collective-permute-start | bytes 196616 | tf_op jit(solution)/shard_map/ppermute | solution.py:139
  140.2 12.1 %collective-permute-start.12 = (f32[1,32,512]{2,1,0:T(8,128)S(1)}, f32[1,32,512]{2,1,0:T(8,128)S(1)}, u32[]{:S(2)}, u32[]{:S(2)}) collective-permute-start(f32[1,32,512]{2,1,0:T(8,128)S(1)} %get-tuple-element.27), channel_id=1, source_target_pairs={{32,0},{64,32},{96,64},{128,96},{160,128},{192,160},{224,192},{33,... | collective-permute-start | bytes 196616 | tf_op jit(solution)/shard_map/ppermute | solution.py:140
  142.1 10.2 %collective-permute-start.13 = (f32[1,32,512]{2,1,0:T(8,128)S(1)}, f32[1,32,512]{2,1,0:T(8,128)S(1)}, u32[]{:S(2)}, u32[]{:S(2)}) collective-permute-start(f32[1,32,512]{2,1,0:T(8,128)S(1)} %get-tuple-element.28), channel_id=1, source_target_pairs={{0,32},{32,64},{64,96},{96,128},{128,160},{160,192},{192,224},{1,3... | collective-permute-start | bytes 196616 | tf_op jit(solution)/shard_map/ppermute | solution.py:139
  146.4 5.9 %collective-permute-start.14 = (f32[32,1,512]{2,1,0:T(1,128)S(1)}, f32[32,1,512]{2,1,0:T(1,128)S(1)}, u32[]{:S(2)}, u32[]{:S(2)}) collective-permute-start(f32[32,1,512]{2,1,0:T(1,128)S(1)} %get-tuple-element.31), channel_id=1, source_target_pairs={{1,0},{2,1},{3,2},{4,3},{5,4},{6,5},{7,6},{8,7},{9,8},{10,9},{11,1... | collective-permute-start | bytes 196616 | tf_op jit(solution)/shard_map/ppermute | solution.py:140
  147.7 5.3 %collective-permute-start.15 = (f32[32,1,512]{2,1,0:T(1,128)S(1)}, f32[32,1,512]{2,1,0:T(1,128)S(1)}, u32[]{:S(2)}, u32[]{:S(2)}) collective-permute-start(f32[32,1,512]{2,1,0:T(1,128)S(1)} %get-tuple-element.32), channel_id=1, source_target_pairs={{0,1},{1,2},{2,3},{3,4},{4,5},{5,6},{6,7},{7,8},{8,9},{9,10},{10,1... | collective-permute-start | bytes 196616 | tf_op jit(solution)/shard_map/ppermute | solution.py:139
  159.5 12.6 %collective-permute-start.16 = (f32[1,32,512]{2,1,0:T(8,128)S(1)}, f32[1,32,512]{2,1,0:T(8,128)S(1)}, u32[]{:S(2)}, u32[]{:S(2)}) collective-permute-start(f32[1,32,512]{2,1,0:T(8,128)S(1)} %get-tuple-element.17), channel_id=1, source_target_pairs={{32,0},{64,32},{96,64},{128,96},{160,128},{192,160},{224,192},{33,... | collective-permute-start | bytes 196616 | tf_op jit(solution)/shard_map/ppermute | solution.py:140
  161.4 10.7 %collective-permute-start.17 = (f32[1,32,512]{2,1,0:T(8,128)S(1)}, f32[1,32,512]{2,1,0:T(8,128)S(1)}, u32[]{:S(2)}, u32[]{:S(2)}) collective-permute-start(f32[1,32,512]{2,1,0:T(8,128)S(1)} %get-tuple-element.18), channel_id=1, source_target_pairs={{0,32},{32,64},{64,96},{96,128},{128,160},{160,192},{192,224},{1,3... | collective-permute-start | bytes 196616 | tf_op jit(solution)/shard_map/ppermute | solution.py:139
  165.4 6.7 %collective-permute-start.18 = (f32[32,1,512]{2,1,0:T(1,128)S(1)}, f32[32,1,512]{2,1,0:T(1,128)S(1)}, u32[]{:S(2)}, u32[]{:S(2)}) collective-permute-start(f32[32,1,512]{2,1,0:T(1,128)S(1)} %get-tuple-element.21), channel_id=1, source_target_pairs={{1,0},{2,1},{3,2},{4,3},{5,4},{6,5},{7,6},{8,7},{9,8},{10,9},{11,1... | collective-permute-start | bytes 196616 | tf_op jit(solution)/shard_map/ppermute | solution.py:140
  166.7 6.1 %collective-permute-start.19 = (f32[32,1,512]{2,1,0:T(1,128)S(1)}, f32[32,1,512]{2,1,0:T(1,128)S(1)}, u32[]{:S(2)}, u32[]{:S(2)}) collective-permute-start(f32[32,1,512]{2,1,0:T(1,128)S(1)} %get-tuple-element.22), channel_id=1, source_target_pairs={{0,1},{1,2},{2,3},{3,4},{4,5},{5,6},{6,7},{7,8},{8,9},{9,10},{10,1... | collective-permute-start | bytes 196616 | tf_op jit(solution)/shard_map/ppermute | solution.py:139
  181.3 2.9 copy-start.11
  189.2 12.6 %copy-start.21 = (s32[8]{0:T(128)S(1)}, s32[8]{0:T(128)}, u32[]{:S(2)}) copy-start(s32[8]{0:T(128)} %param.9) | copy-start | bytes 100
  189.2 112.2 %all-to-all-start = ((f32[32,16,16,128]{3,2,1,0:T(8,128)}), f32[32,16,16,128]{3,2,1,0:T(8,128)}, u32[]{:S(2)}, u32[]{:S(2)}) async-start(f32[32,16,16,128]{3,2,1,0:T(8,128)} %select_select_fusion), calls=%async_computation | async-start | bytes 8388608 | tf_op jit(solution)/shard_map/all_to_all | solution.py:209
